TPU v7x, 128 devices: a whole 4x4x4 slice. The times are simulated.
128 devices in a mesh: slab: 32 (over y, x, core), grp: 4 (over z).
Axes of the slice: x: 4, y: 4, z: 4, core: 2. Of those that a mesh axis runs over, the one named last changes fastest.
Arguments:
- images: float32 [128, 512, 512], P(('slab', 'grp')), may hold values from -6 to 6
- crossing_row: int32 [128, 1024], P(('slab', 'grp')), may hold values from 0 to 511
- crossing_dest: int32 [128, 1024, 1], P(('slab', 'grp')), may hold values from 0 to 127; in each aligned block of 1024 rows (0 to 1023, 1024 to 2047, ..., all dimensions but the last counted through in order) at most 16 rows name the same one
- crossing_line: int32 [128, 1024], P(('slab', 'grp')), may hold values from 0 to 127
- interp_weight: bfloat16 [128, 1024, 16], P(('slab', 'grp')), may hold values from 0 to 1
Outputs:
- reconstruction: float32 [2, 512, 512, 512], P(None, 'slab', 'grp')
Inputs may be any that keep to these rules, and one draw needn't show every extreme that they name: `crossing_dest`: within the rows of one device (1024 crossings), at most 16 crossings name the same destination, and in every draw some destination is named by exactly 16 of them.
All inputs are finite; a program needn't handle non-finite values.
Results may differ from a plain program's by a relative error of at most 0.0029.
Values may be sent and summed in bfloat16 or wider, within the bound.
No kernel may reach another device: no remote copies, remote signals or barrier semaphores. Data moves between devices by JAX's collectives and lax.ppermute only.
A program may use at most 128 MiB of HBM per device.

v0:
```python
import math

import jax
import jax.numpy as jnp
import ml_dtypes
import numpy as np
from jax import lax
from jax.experimental import pallas as pl
from jax.sharding import PartitionSpec as P


def twiddles(length):
    index_grid = np.arange(length)
    phase_angle = (np.outer(index_grid, index_grid) % length) * (2.0 * np.pi / length)
    norm_scale = 1.0 / math.sqrt(length)
    return (np.cos(phase_angle) * norm_scale, np.sin(phase_angle) * norm_scale)


def halves(values):
    high = values.astype(ml_dtypes.bfloat16)
    low = (values - high.astype(np.float64)).astype(ml_dtypes.bfloat16)
    return jnp.asarray(high), jnp.asarray(low)


def accumulate_and_transform(spread_ref, rows_ref, inverse_high_ref, inverse_low_ref, out_ref):
    volume = jnp.dot(spread_ref[...], rows_ref[...], preferred_element_type=jnp.float32)
    volume_high = volume.astype(jnp.bfloat16)
    volume_low = (volume - volume_high.astype(jnp.float32)).astype(jnp.bfloat16)
    contract = (((1,), (1,)), ((), ()))
    along = lax.dot_general(inverse_high_ref[...], volume_high, contract, preferred_element_type=jnp.float32)
    along = along + lax.dot_general(inverse_high_ref[...], volume_low, contract, preferred_element_type=jnp.float32)
    along = along + lax.dot_general(inverse_low_ref[...], volume_high, contract, preferred_element_type=jnp.float32)
    blocks, _, parts, x_in, lanes = out_ref.shape
    for part in range(parts):
        piece = along[:, part * lanes : (part + 1) * lanes].reshape(blocks, 2, x_in, lanes)
        out_ref[:, :, part, :, :] = piece.astype(out_ref.dtype)


def local(images, crossing_row, crossing_dest, crossing_line, interp_weight):
    high = lax.Precision.HIGH
    length = images.shape[1]
    crossings = crossing_row.shape[1]
    slab_count = lax.axis_size("slab")
    group_count = lax.axis_size("grp")
    devices_all = slab_count * group_count
    planes = length // slab_count
    lines_per = length // group_count
    capacity = 2 * crossings // devices_all
    slot_count = devices_all * capacity
    x_block = length // slab_count
    cosine_table, sine_table = twiddles(length)

    image = images[0]
    forward_y = jnp.asarray(np.concatenate([cosine_table, -sine_table], axis=0), jnp.float32)
    along_y = jnp.dot(forward_y, image, precision=high, preferred_element_type=jnp.float32)
    from_real = jnp.asarray(np.concatenate([cosine_table, -sine_table], axis=1), jnp.float32)
    from_imag = jnp.asarray(np.concatenate([sine_table, cosine_table], axis=1), jnp.float32)
    spectra = jnp.dot(along_y[:length], from_real, precision=high, preferred_element_type=jnp.float32)
    spectra = spectra + jnp.dot(along_y[length:], from_imag, precision=high, preferred_element_type=jnp.float32)
    spectra_low = spectra.astype(jnp.bfloat16)

    row_hits = (crossing_row[0][:, None] == jnp.arange(length, dtype=jnp.int32)[None, :]).astype(
        jnp.bfloat16
    )
    slice_rows = jnp.dot(row_hits, spectra_low, preferred_element_type=jnp.float32).astype(jnp.bfloat16)
    extra = 128
    meta_grid = jnp.arange(extra, dtype=jnp.int32)[None, :]
    weight_place = jnp.asarray(np.eye(planes, extra), jnp.bfloat16)
    meta = jnp.dot(interp_weight[0], weight_place, preferred_element_type=jnp.float32)
    meta = meta + jnp.where(meta_grid == planes, crossing_line[0][:, None].astype(jnp.float32), 0.0)
    payload = jnp.concatenate([slice_rows, meta.astype(jnp.bfloat16)], axis=1)

    destination = crossing_dest[0, :, 0]
    onehot = (destination[:, None] == jnp.arange(devices_all, dtype=jnp.int32)[None, :]).astype(jnp.int32)
    earlier = jnp.cumsum(onehot, axis=0) - onehot
    slot_within = jnp.sum(earlier * onehot, axis=1)
    position = destination * capacity + slot_within
    placing = (jnp.arange(slot_count, dtype=jnp.int32)[:, None] == position[None, :]).astype(jnp.bfloat16)
    send = jnp.dot(placing, payload, preferred_element_type=jnp.float32).astype(jnp.bfloat16)
    width = 2 * length + extra
    got = lax.all_to_all(
        send.reshape(devices_all, capacity, width), ("slab", "grp"), split_axis=0, concat_axis=0, tiled=True
    ).reshape(slot_count, width)

    weight_in = got[:, 2 * length : 2 * length + planes]
    line_in = got[:, 2 * length + planes].astype(jnp.float32)
    line_grid = jnp.arange(lines_per, dtype=jnp.float32)[None, :, None]
    spread = jnp.where(
        line_in[None, None, :] == line_grid, weight_in.T[:, None, :], jnp.zeros((), jnp.bfloat16)
    ).reshape(planes * lines_per, slot_count)

    inverse = np.concatenate(
        [
            np.concatenate([cosine_table, sine_table], axis=1),
            np.concatenate([-sine_table, cosine_table], axis=1),
        ],
        axis=0,
    )
    inverse_high, inverse_low = halves(
        inverse.reshape(2 * length, 2, slab_count, x_block).transpose(2, 1, 3, 0).reshape(2 * length, 2 * length)
    )
    step_planes = 2
    step_columns = step_planes * lines_per
    along_x = pl.pallas_call(
        accumulate_and_transform,
        out_shape=jax.ShapeDtypeStruct((slab_count, 2, planes, x_block, lines_per), jnp.bfloat16),
        grid=(planes // step_planes,),
        in_specs=[
            pl.BlockSpec((step_columns, slot_count), lambda i: (i, 0)),
            pl.BlockSpec((slot_count, 2 * length), lambda i: (0, 0)),
            pl.BlockSpec((2 * length, 2 * length), lambda i: (0, 0)),
            pl.BlockSpec((2 * length, 2 * length), lambda i: (0, 0)),
        ],
        out_specs=pl.BlockSpec((slab_count, 2, step_planes, x_block, lines_per), lambda i: (0, 0, i, 0, 0)),
    )(spread, got, inverse_high, inverse_low)
    pencil = lax.all_to_all(along_x, "slab", split_axis=0, concat_axis=0, tiled=True)

    lhs = pencil.transpose(3, 4, 0, 1, 2).reshape(x_block * lines_per, 2 * length)
    z_table = inverse.reshape(2, slab_count, planes, 2 * length).transpose(1, 0, 2, 3).reshape(2 * length, 2 * length)
    z_high, z_low = halves(z_table)
    parts = []
    for part in range(2):
        columns = slice(part * length, (part + 1) * length)
        flat = jnp.dot(lhs, z_high[:, columns], preferred_element_type=jnp.float32)
        flat = flat + jnp.dot(lhs, z_low[:, columns], preferred_element_type=jnp.float32)
        parts.append(flat.reshape(x_block, lines_per, length))
    result = jnp.stack(parts)
    return result


def solution(mesh):
    return jax.shard_map(
        local,
        mesh=mesh,
        in_specs=(
            P(("slab", "grp"), None, None),
            P(("slab", "grp"), None),
            P(("slab", "grp"), None, None),
            P(("slab", "grp"), None),
            P(("slab", "grp"), None, None),
        ),
        out_specs=P(None, "slab", "grp", None),
        check_vma=False,
    )
```

profile of v0, /device:TPU:0, one launch (start us, length us, event | category | flops | bytes accessed | tf_op | source)
XLA Modules:
  0.0 195.0 jit_solution(18228516927518036186)
XLA Ops:
  0.0 0.8 convert_element_type.46
  0.8 0.8 copy.16
  1.6 0.2 fusion.36
  2.0 1.2 fusion.35
  3.2 0.7 multiply_add_fusion
  3.9 3.6 %fusion.31 = f32[1024,512]{1,0:T(8,128)S(1)} fusion(f32[1024,512]{1,0:T(8,128)} %constant.29.clone, f32[1,512,512]{2,1,0:T(8,128)S(1)} %copy-done), kind=kOutput, calls=%fused_computation.33 | convolution fusion | flops 1610612736 | bytes 5242880 | tf_op jit(solution)/shard_map/dot_general | solution.py:55
  7.4 1.9 fusion.29
  9.4 2.0 %add_convert_fusion = bf16[512,1024]{1,0:T(8,128)(2,1)S(1)} fusion(f32[512,1024]{1,0:T(8,128)S(1)} %fusion.29, f32[512,1024]{1,0:T(8,128)S(1)} %copy-done.3, f32[1024,512]{1,0:T(8,128)S(1)} %fusion.31), kind=kOutput, calls=%fused_computation.23 | convolution fusion | flops 1611661312 | bytes 6291456 | tf_op jit(solution)/shard_map/dot_general | solution.py:59
  11.5 1.3 fusion.25
  12.8 0.3 fusion.27
  13.1 6.2 %fusion.1 = bf16[2048,1152]{1,0:T(8,128)(2,1)S(1)} fusion(s32[1024]{0:T(1024)S(1)} %multiply_add_fusion, bf16[1024,128]{1,0:T(8,128)(2,1)S(1)} %fusion.27, bf16[1024,1024]{1,0:T(8,128)(2,1)S(1)} %fusion.25), kind=kOutput, calls=%fused_computation.4 | convolution fusion | flops 4841013248 | bytes 7081984 | tf_op jit(solution)/shard_map/dot_general | solution.py:79
  19.3 69.1 %all_to_all.10 = bf16[128,16,1152]{2,1,0:T(8,128)(2,1)S(1)} all-to-all(bf16[128,16,1152]{2,1,0:T(8,128)(2,1)S(1)} %bitcast.64), channel_id=1, replica_groups=mesh['slab'=32,'grp'=4] {'slab','grp'}, dimensions={0} | all-to-all | bytes 9437184 | tf_op jit(solution)/shard_map/all_to_all | solution.py:81
  88.5 0.4 convert_reduce_fusion
  88.9 1.7 copy-done.2
  90.6 0.2 iota_compare_fusion.8
  90.8 0.2 copy.18
  91.0 4.7 %broadcast_select_fusion = bf16[16,128,2048]{2,1,0:T(8,128)(2,1)} fusion(pred[128,2048]{1,0:T(8,128)(4,1)S(1)} %iota_compare_fusion.8, bf16[16,2048]{1,0:T(8,128)(2,1)S(1)} %copy.18), kind=kLoop, calls=%fused_computation.3 | loop fusion | flops 4194304 | bytes 8716288 | tf_op jit(solution)/shard_map/jit(_where)/select_n | solution.py:88
  95.7 28.8 %shard_map.127 = bf16[32,2,16,16,128]{4,3,2,1,0:T(8,128)(2,1)} custom-call(bf16[2048,2048]{1,0:T(8,128)(2,1)} %bitcast.60, bf16[2048,1152]{1,0:T(8,128)(2,1)} %bitcast.63, bf16[1024,1024]{1,0:T(8,128)(2,1)} %constant.33.clone.inverse_high_ref, bf16[1024,1024]{1,0:T(8,128)(2,1)} %constant.34.clone.inverse_low_ref), custom_call_target="tpu_custom_call" | custom-call | tf_op jit(solution)/shard_map/pallas_call | solution.py:104
  124.5 55.2 %all_to_all.11 = bf16[32,2,16,16,128]{4,3,2,1,0:T(8,128)(2,1)S(1)} all-to-all(bf16[32,2,16,16,128]{4,3,2,1,0:T(8,128)(2,1)} %shard_map.127), channel_id=1, replica_groups=mesh['slab'=32,'grp'=4] {'slab'}, dimensions={0} | all-to-all | bytes 8388608 | tf_op jit(solution)/shard_map/all_to_all | solution.py:116
  179.8 2.5 %fusion.2 = f32[2048,512]{1,0:T(8,128)S(1)} fusion(bf16[1024,512]{1,0:T(8,128)(2,1)S(1)} %copy-done.10, bf16[128,8,16,128]{3,2,1,0:T(8,128)(2,1)S(1)} %bitcast.65), kind=kOutput, calls=%fused_computation.5 | convolution fusion | flops 2147483648 | bytes 9437184 | tf_op jit(solution)/shard_map/dot_general | solution.py:125
  182.3 2.5 %fusion.6 = f32[2048,512]{1,0:T(8,128)S(1)} fusion(bf16[1024,512]{1,0:T(8,128)(2,1)S(1)} %copy-done.9, bf16[128,8,16,128]{3,2,1,0:T(8,128)(2,1)S(1)} %bitcast.66), kind=kOutput, calls=%fused_computation.9 | convolution fusion | flops 2147483648 | bytes 9437184 | tf_op jit(solution)/shard_map/dot_general | solution.py:125
  184.7 2.9 %fusion.14 = f32[2048,512]{1,0:T(8,128)S(1)} fusion(f32[2048,512]{1,0:T(8,128)S(1)} %fusion.2, bf16[1024,512]{1,0:T(8,128)(2,1)S(1)} %copy-done.8, bf16[128,8,16,128]{3,2,1,0:T(8,128)(2,1)S(1)} %bitcast.67), kind=kOutput, calls=%fused_computation.15 | convolution fusion | flops 2148532224 | bytes 13631488 | tf_op jit(solution)/shard_map/dot_general | solution.py:124
  187.6 2.9 %fusion.11 = f32[2048,512]{1,0:T(8,128)S(1)} fusion(f32[2048,512]{1,0:T(8,128)S(1)} %fusion.6, bf16[1024,512]{1,0:T(8,128)(2,1)S(1)} %copy-done.7, bf16[128,8,16,128]{3,2,1,0:T(8,128)(2,1)S(1)} %bitcast.68), kind=kOutput, calls=%fused_computation.14 | convolution fusion | flops 2148532224 | bytes 13631488 | tf_op jit(solution)/shard_map/dot_general | solution.py:124
  190.6 4.4 %pad_maximum_fusion = f32[2,16,128,512]{3,2,1,0:T(8,128)} fusion(f32[1,16,128,512]{3,2,1,0:T(8,128)S(1)} %bitcast.69, f32[1,16,128,512]{3,2,1,0:T(8,128)S(1)} %bitcast.70), kind=kLoop, calls=%fused_computation | loop fusion | flops 2097152 | bytes 16777216 | tf_op jit(solution)/shard_map/stack | solution.py:127
  (30 shorter events, 0.3 us)
Async XLA Ops:
  0.0 3.9 %copy-start = (f32[1,512,512]{2,1,0:T(8,128)S(1)}, f32[1,512,512]{2,1,0:T(8,128)}, u32[]{:S(2)}) copy-start(f32[1,512,512]{2,1,0:T(8,128)} %param.13) | copy-start | bytes 3145732
  1.8 5.6 %copy-start.4 = (f32[512,1024]{1,0:T(8,128)S(1)}, f32[512,1024]{1,0:T(8,128)}, u32[]{:S(2)}) copy-start(f32[512,1024]{1,0:T(8,128)} %constant.30.clone) | copy-start | bytes 6291460
  3.9 5.5 %copy-start.3 = (f32[512,1024]{1,0:T(8,128)S(1)}, f32[512,1024]{1,0:T(8,128)}, u32[]{:S(2)}) copy-start(f32[512,1024]{1,0:T(8,128)} %constant.31.clone) | copy-start | bytes 6291460
  9.4 2.0 %copy-start.6 = (s32[1,1024]{1,0:T(1,128)S(1)}, s32[1,1024]{1,0:T(1,128)}, u32[]{:S(2)}) copy-start(s32[1,1024]{1,0:T(1,128)} %param.14) | copy-start | bytes 12292
  11.5 1.3 copy-start.5
  11.5 1.3 copy-start.11
  88.5 2.1 %copy-start.2 = (bf16[128,16,1152]{2,1,0:T(8,128)(2,1)}, bf16[128,16,1152]{2,1,0:T(8,128)(2,1)S(1)}, u32[]{:S(2)}) copy-start(bf16[128,16,1152]{2,1,0:T(8,128)(2,1)S(1)} %all_to_all.10) | copy-start | bytes 14155780
  124.5 55.2 %copy-start.10 = (bf16[1024,512]{1,0:T(8,128)(2,1)S(1)}, bf16[1024,512]{1,0:T(8,128)(2,1)}, u32[]{:S(2)}) copy-start(bf16[1024,512]{1,0:T(8,128)(2,1)} %constant.45) | copy-start | bytes 3145732
  179.8 2.5 %copy-start.9 = (bf16[1024,512]{1,0:T(8,128)(2,1)S(1)}, bf16[1024,512]{1,0:T(8,128)(2,1)}, u32[]{:S(2)}) copy-start(bf16[1024,512]{1,0:T(8,128)(2,1)} %constant.43) | copy-start | bytes 3145732
  182.2 2.5 %copy-start.8 = (bf16[1024,512]{1,0:T(8,128)(2,1)S(1)}, bf16[1024,512]{1,0:T(8,128)(2,1)}, u32[]{:S(2)}) copy-start(bf16[1024,512]{1,0:T(8,128)(2,1)} %constant.44) | copy-start | bytes 3145732
  184.7 2.9 %copy-start.7 = (bf16[1024,512]{1,0:T(8,128)(2,1)S(1)}, bf16[1024,512]{1,0:T(8,128)(2,1)}, u32[]{:S(2)}) copy-start(bf16[1024,512]{1,0:T(8,128)(2,1)} %constant.42) | copy-start | bytes 3145732
  190.6 4.4 %copy-start.1 = (f32[1,512,512]{2,1,0:T(8,128)S(1)}, f32[1,512,512]{2,1,0:T(8,128)}, u32[]{:S(2)}) copy-start(f32[1,512,512]{2,1,0:T(8,128)} %param.13) | copy-start | bytes 3145732
where the time goes:
time: 196 us; the launch traced here: 195 us
  blocking collectives  124 us (63%)
  Pallas kernels  28.8 us (15%)
  matrix products  26 us (13%)
  other arithmetic  12.6 us (6%)
  local copies, waits for them, and re-layouts  2.89 us (1%)
    all_to_all x1, blocking collectives, local(): lax.all_to_all(send.reshape(devices_all, capacity, width), ('slab', 'grp'...  69.1 us
    all_to_all x1, blocking collectives, local(): lax.all_to_all(along_x, 'slab', split_axis=0, concat_axis=0, tiled=True)  55.2 us
    pallas_call x1, Pallas kernels, local(): pl.pallas_call(accumulate_and_transform, out_shape=jax.ShapeDtypeStruct((...  28.8 us
    dot_general x1, matrix products, local(): jnp.dot(placing, payload, preferred_element_type=jnp.float32)  6.19 us
    dot_general x2, matrix products, local(): flat = jnp.dot(lhs, z_high[:, columns], preferred_element_type=jnp.float32)  5.79 us
    dot_general x2, matrix products, local(): jnp.dot(lhs, z_low[:, columns], preferred_element_type=jnp.float32)  4.92 us
    select_n x1, other arithmetic, local(): jnp.where(line_in[None, None, :] == line_grid, weight_in.T[:, None, :], j...  4.73 us
    another operation x1, other arithmetic, local(): result = jnp.stack(parts)  4.43 us

commit v1 on v0

--- a/solution.py
+++ b/solution.py
@@ -118,13 +118,13 @@
     lhs = pencil.transpose(3, 4, 0, 1, 2).reshape(x_block * lines_per, 2 * length)
     z_table = inverse.reshape(2, slab_count, planes, 2 * length).transpose(1, 0, 2, 3).reshape(2 * length, 2 * length)
     z_high, z_low = halves(z_table)
-    parts = []
-    for part in range(2):
-        columns = slice(part * length, (part + 1) * length)
-        flat = jnp.dot(lhs, z_high[:, columns], preferred_element_type=jnp.float32)
-        flat = flat + jnp.dot(lhs, z_low[:, columns], preferred_element_type=jnp.float32)
-        parts.append(flat.reshape(x_block, lines_per, length))
-    result = jnp.stack(parts)
+    z_high = z_high.reshape(2 * length, 2, length).transpose(1, 0, 2)
+    z_low = z_low.reshape(2 * length, 2, length).transpose(1, 0, 2)
+    both = jnp.broadcast_to(lhs[None], (2,) + lhs.shape)
+    batched = (((2,), (1,)), ((0,), (0,)))
+    flat = lax.dot_general(both, z_high, batched, preferred_element_type=jnp.float32)
+    flat = flat + lax.dot_general(both, z_low, batched, preferred_element_type=jnp.float32)
+    result = flat.reshape(2, x_block, lines_per, length)
     return result
 
 

time: 196 us -> 203 us (1.036)
  local copies, waits for them, and re-layouts: 2.89 us -> 14.6 us
  other arithmetic: 12.6 us -> 6.69 us
    broadcast_in_dim x0 -> x1, local copies, waits for them, and re-layouts: none -> 6.54 us  [local(): both = jnp.broadcast_to(lhs[None], (2,) + lhs.shape)]
    unnamed x24 -> x27, local copies, waits for them, and re-layouts: 1.79 us -> 6.93 us
    another operation x4 -> x3, other arithmetic: 4.7 us -> 0.26 us  [the longest x1 4.43 us: local(): result = jnp.stack(parts)]
    dot_general x4 -> x2, matrix products: 10.7 us -> 13.6 us  [the longest x1 7.11 us: local(): lax.dot_general(both, z_high, batched, preferred_element_type=jnp.float32)]
where the time goes in v1:
time: 203 us; the launch traced here: 202 us
  blocking collectives  124 us (61%)
  Pallas kernels  28.8 us (14%)
  matrix products  27.2 us (13%)
  local copies, waits for them, and re-layouts  14.6 us (7%)
  other arithmetic  6.69 us (3%)
    all_to_all x1, blocking collectives, local(): lax.all_to_all(send.reshape(devices_all, capacity, width), ('slab', 'grp'...  69.1 us
    all_to_all x1, blocking collectives, local(): lax.all_to_all(along_x, 'slab', split_axis=0, concat_axis=0, tiled=True)  55.1 us
    pallas_call x1, Pallas kernels, local(): pl.pallas_call(accumulate_and_transform, out_shape=jax.ShapeDtypeStruct((...  28.8 us
    dot_general x1, matrix products, local(): lax.dot_general(both, z_high, batched, preferred_element_type=jnp.float32)  7.11 us
    unnamed x27, local copies, waits for them, and re-layouts  6.93 us
    broadcast_in_dim x1, local copies, waits for them, and re-layouts, local(): both = jnp.broadcast_to(lhs[None], (2,) + lhs.shape)  6.54 us
    dot_general x1, matrix products, local(): lax.dot_general(both, z_low, batched, preferred_element_type=jnp.float32)  6.49 us
    dot_general x1, matrix products, local(): jnp.dot(placing, payload, preferred_element_type=jnp.float32)  6.18 us

profile of v1, /device:TPU:0, one launch (start us, length us, event | category | flops | bytes accessed | tf_op | source)
XLA Modules:
  0.0 201.7 jit_solution(611728264124372736)
XLA Ops:
  0.0 0.8 convert_element_type.46
  0.8 0.8 copy.17
  1.6 0.2 fusion.25
  1.9 0.1 copy.18
  2.0 0.4 fusion.24
  2.4 1.0 copy-done.6
  3.4 1.8 fusion.20
  5.3 1.9 fusion.18
  7.3 2.0 %add_convert_fusion = bf16[512,1024]{1,0:T(8,128)(2,1)S(1)} fusion(f32[512,1024]{1,0:T(8,128)S(1)} %fusion.18, f32[512,1024]{1,0:T(8,128)S(1)} %copy-done.4, f32[1024,512]{1,0:T(8,128)S(1)} %fusion.20), kind=kOutput, calls=%fused_computation.14 | convolution fusion | flops 1611661312 | bytes 6291456 | tf_op jit(solution)/shard_map/dot_general | solution.py:59
  9.3 1.3 fusion.14
  10.7 0.3 fusion.16
  11.0 6.2 %fusion.1 = bf16[2048,1152]{1,0:T(8,128)(2,1)S(1)} fusion(s32[1024]{0:T(1024)S(1)} %multiply_add_fusion, bf16[1024,128]{1,0:T(8,128)(2,1)S(1)} %fusion.16, bf16[1024,1024]{1,0:T(8,128)(2,1)S(1)} %fusion.14), kind=kOutput, calls=%fused_computation.3 | convolution fusion | flops 4841013248 | bytes 7081984 | tf_op jit(solution)/shard_map/dot_general | solution.py:79
  17.2 69.1 %all_to_all.10 = bf16[128,16,1152]{2,1,0:T(8,128)(2,1)S(1)} all-to-all(bf16[128,16,1152]{2,1,0:T(8,128)(2,1)S(1)} %bitcast.53), channel_id=1, replica_groups=mesh['slab'=32,'grp'=4] {'slab','grp'}, dimensions={0} | all-to-all | bytes 9437184 | tf_op jit(solution)/shard_map/all_to_all | solution.py:81
  86.3 0.4 convert_reduce_fusion
  86.7 1.7 copy-done.2
  88.4 0.2 iota_compare_fusion.8
  88.6 0.2 copy.19
  88.8 4.7 %broadcast_select_fusion = bf16[16,128,2048]{2,1,0:T(8,128)(2,1)} fusion(pred[128,2048]{1,0:T(8,128)(4,1)S(1)} %iota_compare_fusion.8, bf16[16,2048]{1,0:T(8,128)(2,1)S(1)} %copy.19), kind=kLoop, calls=%fused_computation.2 | loop fusion | flops 4194304 | bytes 8716288 | tf_op jit(solution)/shard_map/jit(_where)/select_n | solution.py:88
  93.5 28.8 %shard_map.127 = bf16[32,2,16,16,128]{4,3,2,1,0:T(8,128)(2,1)} custom-call(bf16[2048,2048]{1,0:T(8,128)(2,1)} %bitcast.47, bf16[2048,1152]{1,0:T(8,128)(2,1)} %bitcast.50, bf16[1024,1024]{1,0:T(8,128)(2,1)} %constant.33.clone.inverse_high_ref, bf16[1024,1024]{1,0:T(8,128)(2,1)} %constant.34.clone.inverse_low_ref), custom_call_target="tpu_custom_call" | custom-call | tf_op jit(solution)/shard_map/pallas_call | solution.py:104
  122.3 55.1 %all_to_all.11 = bf16[32,2,16,16,128]{4,3,2,1,0:T(8,128)(2,1)S(1)} all-to-all(bf16[32,2,16,16,128]{4,3,2,1,0:T(8,128)(2,1)} %shard_map.127), channel_id=1, replica_groups=mesh['slab'=32,'grp'=4] {'slab'}, dimensions={0} | all-to-all | bytes 8388608 | tf_op jit(solution)/shard_map/all_to_all | solution.py:116
  177.4 4.1 %copy.23 = bf16[128,8,16,128]{3,1,2,0:T(8,128)(2,1)} copy(bf16[128,8,16,128]{3,2,1,0:T(8,128)(2,1)S(1)} %bitcast.51) | data formatting | bytes 8388608
  181.5 6.5 %copy.20 = bf16[2048,1024]{1,0:T(8,128)(2,1)} copy(bf16[2048,1024]{0,1:T(8,128)(2,1)} %bitcast.52) | data formatting | bytes 8388608 | tf_op jit(solution)/shard_map/broadcast_in_dim | solution.py:123
  188.1 6.5 %fusion.2 = f32[2,2048,512]{2,1,0:T(8,128)S(1)} fusion(bf16[2,1024,512]{2,1,0:T(8,128)(2,1)S(1)} %copy-done.11, bf16[2048,1024]{1,0:T(8,128)(2,1)} %copy.20), kind=kOutput, calls=%fused_computation.5 | convolution fusion | flops 4294967296 | bytes 14680064 | tf_op jit(solution)/shard_map/dot_general | solution.py:126
  194.6 7.1 %fusion.7 = f32[2,2048,512]{2,1,0:T(8,128)} fusion(f32[2,2048,512]{2,1,0:T(8,128)S(1)} %fusion.2, bf16[2,1024,512]{2,1,0:T(8,128)(2,1)S(1)} %copy-done.10, bf16[2048,1024]{1,0:T(8,128)(2,1)S(1)} %copy-done.3), kind=kOutput, calls=%fused_computation.10 | convolution fusion | flops 4297064448 | bytes 23068672 | tf_op jit(solution)/shard_map/dot_general | solution.py:125
  (31 shorter events, 0.2 us)
Async XLA Ops:
  0.0 2.4 %copy-start = (f32[1,512,512]{2,1,0:T(8,128)S(1)}, f32[1,512,512]{2,1,0:T(8,128)}, u32[]{:S(2)}) copy-start(f32[1,512,512]{2,1,0:T(8,128)} %param.13) | copy-start | bytes 3145732
  0.0 2.0 copy-start.7
  1.8 1.6 copy-start.6
  3.4 1.8 copy-start.5
  5.3 2.0 copy-start.4
  7.2 2.0 %copy-start.9 = (s32[1,1024]{1,0:T(1,128)S(1)}, s32[1,1024]{1,0:T(1,128)}, u32[]{:S(2)}) copy-start(s32[1,1024]{1,0:T(1,128)} %param.14) | copy-start | bytes 12292
  9.3 1.3 copy-start.8
  9.3 1.3 copy-start.12
  86.3 2.1 %copy-start.2 = (bf16[128,16,1152]{2,1,0:T(8,128)(2,1)}, bf16[128,16,1152]{2,1,0:T(8,128)(2,1)S(1)}, u32[]{:S(2)}) copy-start(bf16[128,16,1152]{2,1,0:T(8,128)(2,1)S(1)} %all_to_all.10) | copy-start | bytes 14155780
  181.5 6.5 %copy-start.11 = (bf16[2,1024,512]{2,1,0:T(8,128)(2,1)S(1)}, bf16[2,1024,512]{2,1,0:T(8,128)(2,1)}, u32[]{:S(2)}) copy-start(bf16[2,1024,512]{2,1,0:T(8,128)(2,1)} %constant.45) | copy-start | bytes 6291460
  188.1 6.5 %copy-start.3 = (bf16[2048,1024]{1,0:T(8,128)(2,1)S(1)}, bf16[2048,1024]{1,0:T(8,128)(2,1)}, u32[]{:S(2)}) copy-start(bf16[2048,1024]{1,0:T(8,128)(2,1)} %copy.20) | copy-start | bytes 12582916
  188.1 6.5 %copy-start.10 = (bf16[2,1024,512]{2,1,0:T(8,128)(2,1)S(1)}, bf16[2,1024,512]{2,1,0:T(8,128)(2,1)}, u32[]{:S(2)}) copy-start(bf16[2,1024,512]{2,1,0:T(8,128)(2,1)} %constant.43) | copy-start | bytes 6291460
  194.6 7.1 %copy-start.1 = (f32[1,512,512]{2,1,0:T(8,128)S(1)}, f32[1,512,512]{2,1,0:T(8,128)}, u32[]{:S(2)}) copy-start(f32[1,512,512]{2,1,0:T(8,128)} %param.13) | copy-start | bytes 3145732

commit v2 on v0

--- a/solution.py
+++ b/solution.py
@@ -22,8 +22,14 @@
     return jnp.asarray(high), jnp.asarray(low)
 
 
-def accumulate_and_transform(spread_ref, rows_ref, inverse_high_ref, inverse_low_ref, out_ref):
-    volume = jnp.dot(spread_ref[...], rows_ref[...], preferred_element_type=jnp.float32)
+def accumulate_and_transform(weight_ref, line_ref, rows_ref, inverse_high_ref, inverse_low_ref, out_ref):
+    weights = weight_ref[0]
+    lines = out_ref.shape[-1]
+    hit = line_ref[...] == lax.broadcasted_iota(jnp.int32, (lines, weights.shape[1]), 0)
+    spread = jnp.concatenate(
+        [jnp.where(hit, weights[plane : plane + 1, :], 0.0) for plane in range(weights.shape[0])], axis=0
+    )
+    volume = jnp.dot(spread.astype(jnp.bfloat16), rows_ref[...], preferred_element_type=jnp.float32)
     volume_high = volume.astype(jnp.bfloat16)
     volume_low = (volume - volume_high.astype(jnp.float32)).astype(jnp.bfloat16)
     contract = (((1,), (1,)), ((), ()))
@@ -82,12 +88,11 @@
         send.reshape(devices_all, capacity, width), ("slab", "grp"), split_axis=0, concat_axis=0, tiled=True
     ).reshape(slot_count, width)
 
-    weight_in = got[:, 2 * length : 2 * length + planes]
-    line_in = got[:, 2 * length + planes].astype(jnp.float32)
-    line_grid = jnp.arange(lines_per, dtype=jnp.float32)[None, :, None]
-    spread = jnp.where(
-        line_in[None, None, :] == line_grid, weight_in.T[:, None, :], jnp.zeros((), jnp.bfloat16)
-    ).reshape(planes * lines_per, slot_count)
+    step_planes = 2
+    weight_in = (
+        got[:, 2 * length : 2 * length + planes].T.astype(jnp.float32).reshape(planes // step_planes, step_planes, slot_count)
+    )
+    line_in = got[:, 2 * length + planes].astype(jnp.int32).reshape(1, slot_count)
 
     inverse = np.concatenate(
         [
@@ -99,20 +104,19 @@
     inverse_high, inverse_low = halves(
         inverse.reshape(2 * length, 2, slab_count, x_block).transpose(2, 1, 3, 0).reshape(2 * length, 2 * length)
     )
-    step_planes = 2
-    step_columns = step_planes * lines_per
     along_x = pl.pallas_call(
         accumulate_and_transform,
         out_shape=jax.ShapeDtypeStruct((slab_count, 2, planes, x_block, lines_per), jnp.bfloat16),
         grid=(planes // step_planes,),
         in_specs=[
-            pl.BlockSpec((step_columns, slot_count), lambda i: (i, 0)),
+            pl.BlockSpec((1, step_planes, slot_count), lambda i: (i, 0, 0)),
+            pl.BlockSpec((1, slot_count), lambda i: (0, 0)),
             pl.BlockSpec((slot_count, 2 * length), lambda i: (0, 0)),
             pl.BlockSpec((2 * length, 2 * length), lambda i: (0, 0)),
             pl.BlockSpec((2 * length, 2 * length), lambda i: (0, 0)),
         ],
         out_specs=pl.BlockSpec((slab_count, 2, step_planes, x_block, lines_per), lambda i: (0, 0, i, 0, 0)),
-    )(spread, got, inverse_high, inverse_low)
+    )(weight_in, line_in, got, inverse_high, inverse_low)
     pencil = lax.all_to_all(along_x, "slab", split_axis=0, concat_axis=0, tiled=True)
 
     lhs = pencil.transpose(3, 4, 0, 1, 2).reshape(x_block * lines_per, 2 * length)

time: 196 us -> 192 us (0.980)
  other arithmetic: 12.6 us -> 8.83 us
    select_n x1 -> x0, other arithmetic: 4.73 us -> none  [local(): jnp.where(line_in[None, None, :] == line_grid, weight_in.T[:, None, :], j...]
where the time goes in v2:
time: 192 us; the launch traced here: 191 us
  blocking collectives  124 us (65%)
  Pallas kernels  28.5 us (15%)
  matrix products  26 us (14%)
  other arithmetic  8.83 us (5%)
  local copies, waits for them, and re-layouts  2.76 us (1%)
    all_to_all x1, blocking collectives, local(): lax.all_to_all(send.reshape(devices_all, capacity, width), ('slab', 'grp'...  69.1 us
    all_to_all x1, blocking collectives, local(): lax.all_to_all(along_x, 'slab', split_axis=0, concat_axis=0, tiled=True)  55.2 us
    pallas_call x1, Pallas kernels, local(): pl.pallas_call(accumulate_and_transform, out_shape=jax.ShapeDtypeStruct((...  28.5 us
    dot_general x1, matrix products, local(): jnp.dot(placing, payload, preferred_element_type=jnp.float32)  6.19 us
    dot_general x2, matrix products, local(): flat = jnp.dot(lhs, z_high[:, columns], preferred_element_type=jnp.float32)  5.79 us
    dot_general x2, matrix products, local(): jnp.dot(lhs, z_low[:, columns], preferred_element_type=jnp.float32)  4.92 us
    another operation x1, other arithmetic, local(): result = jnp.stack(parts)  4.43 us

profile of v2, /device:TPU:0, one launch (start us, length us, event | category | flops | bytes accessed | tf_op | source)
XLA Modules:
  0.0 190.8 jit_solution(6263328046475401774)
XLA Ops:
  0.0 0.8 convert_element_type.53
  0.8 0.8 copy.16
  1.6 0.2 fusion.36
  1.9 0.1 copy.17
  2.0 1.2 fusion.35
  3.2 0.7 multiply_add_fusion
  3.9 3.6 %fusion.31 = f32[1024,512]{1,0:T(8,128)S(1)} fusion(f32[1024,512]{1,0:T(8,128)} %constant.27.clone, f32[1,512,512]{2,1,0:T(8,128)S(1)} %copy-done), kind=kOutput, calls=%fused_computation.32 | convolution fusion | flops 1610612736 | bytes 5242880 | tf_op jit(solution)/shard_map/dot_general | solution.py:61
  7.4 1.9 %fusion.29 = f32[512,1024]{1,0:T(8,128)S(1)} fusion(f32[512,1024]{1,0:T(8,128)S(1)} %copy-done.4, f32[1024,512]{1,0:T(8,128)S(1)} %fusion.31), kind=kOutput, calls=%fused_computation.30 | convolution fusion | flops 1610612736 | bytes 5242880 | tf_op jit(solution)/shard_map/dot_general | solution.py:64
  9.4 2.0 %add_convert_fusion = bf16[512,1024]{1,0:T(8,128)(2,1)S(1)} fusion(f32[512,1024]{1,0:T(8,128)S(1)} %fusion.29, f32[512,1024]{1,0:T(8,128)S(1)} %copy-done.3, f32[1024,512]{1,0:T(8,128)S(1)} %fusion.31), kind=kOutput, calls=%fused_computation.22 | convolution fusion | flops 1611661312 | bytes 6291456 | tf_op jit(solution)/shard_map/dot_general | solution.py:65
  11.5 1.3 fusion.25
  12.8 0.3 fusion.27
  13.1 6.2 %fusion.1 = bf16[2048,1152]{1,0:T(8,128)(2,1)S(1)} fusion(s32[1024]{0:T(1024)S(1)} %multiply_add_fusion, bf16[1024,128]{1,0:T(8,128)(2,1)S(1)} %fusion.27, bf16[1024,1024]{1,0:T(8,128)(2,1)S(1)} %fusion.25), kind=kOutput, calls=%fused_computation.3 | convolution fusion | flops 4841013248 | bytes 7081984 | tf_op jit(solution)/shard_map/dot_general | solution.py:85
  19.3 69.1 %all_to_all.10 = bf16[128,16,1152]{2,1,0:T(8,128)(2,1)S(1)} all-to-all(bf16[128,16,1152]{2,1,0:T(8,128)(2,1)S(1)} %bitcast.63), channel_id=1, replica_groups=mesh['slab'=32,'grp'=4] {'slab','grp'}, dimensions={0} | all-to-all | bytes 9437184 | tf_op jit(solution)/shard_map/all_to_all | solution.py:87
  88.5 1.4 convert_reduce_fusion
  89.9 0.8 copy-done.2
  90.7 0.3 copy.18
  91.0 0.7 reshape.73.weight_ref
  91.8 28.5 %shard_map.127 = bf16[32,2,16,16,128]{4,3,2,1,0:T(8,128)(2,1)} custom-call(f32[8,2,2048]{2,1,0:T(2,128)} %reshape.73.weight_ref, s32[1,2048]{1,0:T(1,128)} %bitcast.73, bf16[2048,1152]{1,0:T(8,128)(2,1)} %bitcast.62, bf16[1024,1024]{1,0:T(8,128)(2,1)} %constant.31.clone.inverse_high_ref, bf16[1024,1024]{1,0:T(8,128)(2,1)} %constant.32.clone.inverse_low_ref), custom_call_target="tpu_custom_call" | custom-call | tf_op jit(solution)/shard_map/pallas_call | solution.py:107
  120.3 55.2 %all_to_all.11 = bf16[32,2,16,16,128]{4,3,2,1,0:T(8,128)(2,1)S(1)} all-to-all(bf16[32,2,16,16,128]{4,3,2,1,0:T(8,128)(2,1)} %shard_map.127), channel_id=1, replica_groups=mesh['slab'=32,'grp'=4] {'slab'}, dimensions={0} | all-to-all | bytes 8388608 | tf_op jit(solution)/shard_map/all_to_all | solution.py:120
  175.5 2.5 %fusion.2 = f32[2048,512]{1,0:T(8,128)S(1)} fusion(bf16[1024,512]{1,0:T(8,128)(2,1)S(1)} %copy-done.10, bf16[128,8,16,128]{3,2,1,0:T(8,128)(2,1)S(1)} %bitcast.64), kind=kOutput, calls=%fused_computation.4 | convolution fusion | flops 2147483648 | bytes 9437184 | tf_op jit(solution)/shard_map/dot_general | solution.py:129
  178.0 2.5 %fusion.6 = f32[2048,512]{1,0:T(8,128)S(1)} fusion(bf16[1024,512]{1,0:T(8,128)(2,1)S(1)} %copy-done.9, bf16[128,8,16,128]{3,2,1,0:T(8,128)(2,1)S(1)} %bitcast.65), kind=kOutput, calls=%fused_computation.8 | convolution fusion | flops 2147483648 | bytes 9437184 | tf_op jit(solution)/shard_map/dot_general | solution.py:129
  180.5 2.9 %fusion.14 = f32[2048,512]{1,0:T(8,128)S(1)} fusion(f32[2048,512]{1,0:T(8,128)S(1)} %fusion.2, bf16[1024,512]{1,0:T(8,128)(2,1)S(1)} %copy-done.8, bf16[128,8,16,128]{3,2,1,0:T(8,128)(2,1)S(1)} %bitcast.66), kind=kOutput, calls=%fused_computation.14 | convolution fusion | flops 2148532224 | bytes 13631488 | tf_op jit(solution)/shard_map/dot_general | solution.py:128
  183.4 2.9 %fusion.11 = f32[2048,512]{1,0:T(8,128)S(1)} fusion(f32[2048,512]{1,0:T(8,128)S(1)} %fusion.6, bf16[1024,512]{1,0:T(8,128)(2,1)S(1)} %copy-done.7, bf16[128,8,16,128]{3,2,1,0:T(8,128)(2,1)S(1)} %bitcast.67), kind=kOutput, calls=%fused_computation.13 | convolution fusion | flops 2148532224 | bytes 13631488 | tf_op jit(solution)/shard_map/dot_general | solution.py:128
  186.3 4.4 %pad_maximum_fusion = f32[2,16,128,512]{3,2,1,0:T(8,128)} fusion(f32[1,16,128,512]{3,2,1,0:T(8,128)S(1)} %bitcast.68, f32[1,16,128,512]{3,2,1,0:T(8,128)S(1)} %bitcast.69), kind=kLoop, calls=%fused_computation | loop fusion | flops 2097152 | bytes 16777216 | tf_op jit(solution)/shard_map/stack | solution.py:131
  (29 shorter events, 0.2 us)
Async XLA Ops:
  0.0 3.9 %copy-start = (f32[1,512,512]{2,1,0:T(8,128)S(1)}, f32[1,512,512]{2,1,0:T(8,128)}, u32[]{:S(2)}) copy-start(f32[1,512,512]{2,1,0:T(8,128)} %param.13) | copy-start | bytes 3145732
  1.8 5.6 %copy-start.4 = (f32[512,1024]{1,0:T(8,128)S(1)}, f32[512,1024]{1,0:T(8,128)}, u32[]{:S(2)}) copy-start(f32[512,1024]{1,0:T(8,128)} %constant.28.clone) | copy-start | bytes 6291460
  3.9 5.5 %copy-start.3 = (f32[512,1024]{1,0:T(8,128)S(1)}, f32[512,1024]{1,0:T(8,128)}, u32[]{:S(2)}) copy-start(f32[512,1024]{1,0:T(8,128)} %constant.29.clone) | copy-start | bytes 6291460
  9.4 2.0 %copy-start.6 = (s32[1,1024]{1,0:T(1,128)S(1)}, s32[1,1024]{1,0:T(1,128)}, u32[]{:S(2)}) copy-start(s32[1,1024]{1,0:T(1,128)} %param.14) | copy-start | bytes 12292
  11.5 1.3 copy-start.5
  11.5 1.3 copy-start.11
  88.5 2.2 %copy-start.2 = (bf16[128,16,1152]{2,1,0:T(8,128)(2,1)}, bf16[128,16,1152]{2,1,0:T(8,128)(2,1)S(1)}, u32[]{:S(2)}) copy-start(bf16[128,16,1152]{2,1,0:T(8,128)(2,1)S(1)} %all_to_all.10) | copy-start | bytes 14155780
  120.3 55.2 %copy-start.10 = (bf16[1024,512]{1,0:T(8,128)(2,1)S(1)}, bf16[1024,512]{1,0:T(8,128)(2,1)}, u32[]{:S(2)}) copy-start(bf16[1024,512]{1,0:T(8,128)(2,1)} %constant.43) | copy-start | bytes 3145732
  175.5 2.5 %copy-start.9 = (bf16[1024,512]{1,0:T(8,128)(2,1)S(1)}, bf16[1024,512]{1,0:T(8,128)(2,1)}, u32[]{:S(2)}) copy-start(bf16[1024,512]{1,0:T(8,128)(2,1)} %constant.41) | copy-start | bytes 3145732
  178.0 2.5 %copy-start.8 = (bf16[1024,512]{1,0:T(8,128)(2,1)S(1)}, bf16[1024,512]{1,0:T(8,128)(2,1)}, u32[]{:S(2)}) copy-start(bf16[1024,512]{1,0:T(8,128)(2,1)} %constant.42) | copy-start | bytes 3145732
  180.5 2.9 %copy-start.7 = (bf16[1024,512]{1,0:T(8,128)(2,1)S(1)}, bf16[1024,512]{1,0:T(8,128)(2,1)}, u32[]{:S(2)}) copy-start(bf16[1024,512]{1,0:T(8,128)(2,1)} %constant.40) | copy-start | bytes 3145732
  186.3 4.4 %copy-start.1 = (f32[1,512,512]{2,1,0:T(8,128)S(1)}, f32[1,512,512]{2,1,0:T(8,128)}, u32[]{:S(2)}) copy-start(f32[1,512,512]{2,1,0:T(8,128)} %param.13) | copy-start | bytes 3145732

commit v3 on v2

--- a/solution.py
+++ b/solution.py
@@ -40,6 +40,15 @@
     for part in range(parts):
         piece = along[:, part * lanes : (part + 1) * lanes].reshape(blocks, 2, x_in, lanes)
         out_ref[:, :, part, :, :] = piece.astype(out_ref.dtype)
+
+
+def along_z(lhs_ref, z_high_ref, z_low_ref, out_ref):
+    rows = lhs_ref[...]
+    total = jnp.dot(rows, z_high_ref[...], preferred_element_type=jnp.float32)
+    total = total + jnp.dot(rows, z_low_ref[...], preferred_element_type=jnp.float32)
+    length = out_ref.shape[-1]
+    out_ref[0, 0] = total[:, :length]
+    out_ref[1, 0] = total[:, length:]
 
 
 def local(images, crossing_row, crossing_dest, crossing_line, interp_weight):
@@ -122,13 +131,17 @@
     lhs = pencil.transpose(3, 4, 0, 1, 2).reshape(x_block * lines_per, 2 * length)
     z_table = inverse.reshape(2, slab_count, planes, 2 * length).transpose(1, 0, 2, 3).reshape(2 * length, 2 * length)
     z_high, z_low = halves(z_table)
-    parts = []
-    for part in range(2):
-        columns = slice(part * length, (part + 1) * length)
-        flat = jnp.dot(lhs, z_high[:, columns], preferred_element_type=jnp.float32)
-        flat = flat + jnp.dot(lhs, z_low[:, columns], preferred_element_type=jnp.float32)
-        parts.append(flat.reshape(x_block, lines_per, length))
-    result = jnp.stack(parts)
+    result = pl.pallas_call(
+        along_z,
+        out_shape=jax.ShapeDtypeStruct((2, x_block, lines_per, length), jnp.float32),
+        grid=(x_block,),
+        in_specs=[
+            pl.BlockSpec((lines_per, 2 * length), lambda i: (i, 0)),
+            pl.BlockSpec((2 * length, 2 * length), lambda i: (0, 0)),
+            pl.BlockSpec((2 * length, 2 * length), lambda i: (0, 0)),
+        ],
+        out_specs=pl.BlockSpec((2, 1, lines_per, length), lambda i: (0, i, 0, 0)),
+    )(lhs, z_high, z_low)
     return result
 
 

time: 192 us -> 203 us (1.057)
  Pallas kernels: 28.5 us -> 46.4 us
  matrix products: 26 us -> 13.6 us
  local copies, waits for them, and re-layouts: 2.76 us -> 14.2 us
  other arithmetic: 8.83 us -> 2.95 us
    pallas_call x0 -> x1, Pallas kernels: none -> 17.9 us  [local(): pl.pallas_call(along_z, out_shape=jax.ShapeDtypeStruct((2, x_block, lines...]
    dot_general x4 -> x0, matrix products: 10.7 us -> none  [the longest x2 5.79 us: local(): flat = jnp.dot(lhs, z_high[:, columns], preferred_element_type=jnp.float32)]
    reshape x0 -> x1, local copies, waits for them, and re-layouts: none -> 6.4 us  [local(): pencil.transpose(3, 4, 0, 1, 2).reshape(x_block * lines_per, 2 * length)]
    unnamed x24 -> x19, local copies, waits for them, and re-layouts: 0.82 us -> 5.92 us
    another operation x4 -> x3, other arithmetic: 4.7 us -> 0.26 us  [the longest x1 4.43 us: local(): result = jnp.stack(parts)]
where the time goes in v3:
time: 203 us; the launch traced here: 202 us
  blocking collectives  124 us (61%)
  Pallas kernels  46.4 us (23%)
  local copies, waits for them, and re-layouts  14.2 us (7%)
  matrix products  13.6 us (7%)
  other arithmetic  2.95 us (1%)
    all_to_all x1, blocking collectives, local(): lax.all_to_all(send.reshape(devices_all, capacity, width), ('slab', 'grp'...  69.1 us
    all_to_all x1, blocking collectives, local(): lax.all_to_all(along_x, 'slab', split_axis=0, concat_axis=0, tiled=True)  55.1 us
    pallas_call x1, Pallas kernels, local(): pl.pallas_call(accumulate_and_transform, out_shape=jax.ShapeDtypeStruct((...  28.5 us
    pallas_call x1, Pallas kernels, local(): pl.pallas_call(along_z, out_shape=jax.ShapeDtypeStruct((2, x_block, lines...  17.9 us
    reshape x1, local copies, waits for them, and re-layouts, local(): pencil.transpose(3, 4, 0, 1, 2).reshape(x_block * lines_per, 2 * length)  6.4 us
    dot_general x1, matrix products, local(): jnp.dot(placing, payload, preferred_element_type=jnp.float32)  6.19 us
    unnamed x19, local copies, waits for them, and re-layouts  5.92 us

profile of v3, /device:TPU:0, one launch (start us, length us, event | category | flops | bytes accessed | tf_op | source)
XLA Modules:
  0.0 201.6 jit_solution(17620064661918061685)
XLA Ops:
  0.0 0.8 convert_element_type.53
  0.8 0.8 copy.17
  1.6 0.2 fusion.18
  1.9 0.1 copy.18
  2.0 0.4 fusion.17
  2.4 1.0 copy-done.4
  3.4 1.8 fusion.13
  5.3 0.0 copy-start.2
  5.3 1.9 fusion.11
  7.3 2.0 %add_convert_fusion = bf16[512,1024]{1,0:T(8,128)(2,1)S(1)} fusion(f32[512,1024]{1,0:T(8,128)S(1)} %fusion.11, f32[512,1024]{1,0:T(8,128)S(1)} %copy-done.2, f32[1024,512]{1,0:T(8,128)S(1)} %fusion.13), kind=kOutput, calls=%fused_computation.8 | convolution fusion | flops 1611661312 | bytes 6291456 | tf_op jit(solution)/shard_map/dot_general | solution.py:74
  9.3 1.3 fusion.7
  10.7 0.3 fusion.9
  11.0 6.2 %fusion.1 = bf16[2048,1152]{1,0:T(8,128)(2,1)S(1)} fusion(s32[1024]{0:T(1024)S(1)} %multiply_add_fusion, bf16[1024,128]{1,0:T(8,128)(2,1)S(1)} %fusion.9, bf16[1024,1024]{1,0:T(8,128)(2,1)S(1)} %fusion.7), kind=kOutput, calls=%fused_computation.2 | convolution fusion | flops 4841013248 | bytes 7081984 | tf_op jit(solution)/shard_map/dot_general | solution.py:94
  17.2 69.1 %all_to_all.10 = bf16[128,16,1152]{2,1,0:T(8,128)(2,1)S(1)} all-to-all(bf16[128,16,1152]{2,1,0:T(8,128)(2,1)S(1)} %bitcast.49), channel_id=1, replica_groups=mesh['slab'=32,'grp'=4] {'slab','grp'}, dimensions={0} | all-to-all | bytes 9437184 | tf_op jit(solution)/shard_map/all_to_all | solution.py:96
  86.3 1.5 convert_reduce_fusion
  87.8 0.7 copy-done.1
  88.5 0.1 convert_bitcast_fusion
  88.6 0.3 copy.19
  88.9 0.7 reshape.73.weight_ref
  89.6 28.5 %shard_map.127 = bf16[32,2,16,16,128]{4,3,2,1,0:T(8,128)(2,1)} custom-call(f32[8,2,2048]{2,1,0:T(2,128)} %reshape.73.weight_ref, s32[1,2048]{1,0:T(1,128)} %bitcast.53, bf16[2048,1152]{1,0:T(8,128)(2,1)} %bitcast.46, bf16[1024,1024]{1,0:T(8,128)(2,1)} %constant.31.clone.inverse_high_ref, bf16[1024,1024]{1,0:T(8,128)(2,1)} %constant.32.clone.inverse_low_ref), custom_call_target="tpu_custom_call" | custom-call | tf_op jit(solution)/shard_map/pallas_call | solution.py:116
  118.1 55.1 %all_to_all.11 = bf16[32,2,16,16,128]{4,3,2,1,0:T(8,128)(2,1)S(1)} all-to-all(bf16[32,2,16,16,128]{4,3,2,1,0:T(8,128)(2,1)} %shard_map.127), channel_id=1, replica_groups=mesh['slab'=32,'grp'=4] {'slab'}, dimensions={0} | all-to-all | bytes 8388608 | tf_op jit(solution)/shard_map/all_to_all | solution.py:129
  173.2 4.1 %copy.23 = bf16[128,8,16,128]{3,1,2,0:T(8,128)(2,1)} copy(bf16[128,8,16,128]{3,2,1,0:T(8,128)(2,1)S(1)} %bitcast.47) | data formatting | bytes 8388608
  177.3 6.4 %copy.20.lhs_ref = bf16[2048,1024]{1,0:T(8,128)(2,1)} copy(bf16[2048,1024]{0,1:T(8,128)(2,1)} %bitcast.48) | data formatting | bytes 8388608 | tf_op jit(solution)/shard_map/reshape | solution.py:131
  183.7 17.9 %shard_map.128 = f32[2,16,128,512]{3,2,1,0:T(8,128)} custom-call(bf16[2048,1024]{1,0:T(8,128)(2,1)} %copy.20.lhs_ref, bf16[1024,1024]{1,0:T(8,128)(2,1)} %constant.33.clone.z_high_ref, bf16[1024,1024]{1,0:T(8,128)(2,1)} %constant.34.clone.z_low_ref), custom_call_target="tpu_custom_call" | custom-call | tf_op jit(solution)/shard_map/pallas_call | solution.py:134
  (21 shorter events, 0.1 us)
Async XLA Ops:
  0.0 2.4 %copy-start = (f32[1,512,512]{2,1,0:T(8,128)S(1)}, f32[1,512,512]{2,1,0:T(8,128)}, u32[]{:S(2)}) copy-start(f32[1,512,512]{2,1,0:T(8,128)} %param.13) | copy-start | bytes 3145732
  0.0 2.0 copy-start.5
  1.8 1.6 copy-start.4
  3.4 1.9 copy-start.3
  5.3 2.0 copy-start.2
  7.3 2.0 %copy-start.7 = (s32[1,1024]{1,0:T(1,128)S(1)}, s32[1,1024]{1,0:T(1,128)}, u32[]{:S(2)}) copy-start(s32[1,1024]{1,0:T(1,128)} %param.14) | copy-start | bytes 12292
  9.3 1.3 copy-start.6
  9.3 1.3 copy-start.8
  86.3 2.2 %copy-start.1 = (bf16[128,16,1152]{2,1,0:T(8,128)(2,1)}, bf16[128,16,1152]{2,1,0:T(8,128)(2,1)S(1)}, u32[]{:S(2)}) copy-start(bf16[128,16,1152]{2,1,0:T(8,128)(2,1)S(1)} %all_to_all.10) | copy-start | bytes 14155780

commit v4 on v3

--- a/solution.py
+++ b/solution.py
@@ -42,13 +42,14 @@
         out_ref[:, :, part, :, :] = piece.astype(out_ref.dtype)
 
 
-def along_z(lhs_ref, z_high_ref, z_low_ref, out_ref):
-    rows = lhs_ref[...]
-    total = jnp.dot(rows, z_high_ref[...], preferred_element_type=jnp.float32)
-    total = total + jnp.dot(rows, z_low_ref[...], preferred_element_type=jnp.float32)
-    length = out_ref.shape[-1]
-    out_ref[0, 0] = total[:, :length]
-    out_ref[1, 0] = total[:, length:]
+def along_z(z_high_ref, z_low_ref, pencil_ref, out_ref):
+    columns = pencil_ref[...]
+    total = jnp.dot(z_high_ref[...], columns, preferred_element_type=jnp.float32)
+    total = total + jnp.dot(z_low_ref[...], columns, preferred_element_type=jnp.float32)
+    _, xs, lines, length = out_ref.shape
+    for part in range(2):
+        for x in range(xs):
+            out_ref[part, x] = total[part * length : (part + 1) * length, x * lines : (x + 1) * lines].T
 
 
 def local(images, crossing_row, crossing_dest, crossing_line, interp_weight):
@@ -128,20 +129,21 @@
     )(weight_in, line_in, got, inverse_high, inverse_low)
     pencil = lax.all_to_all(along_x, "slab", split_axis=0, concat_axis=0, tiled=True)
 
-    lhs = pencil.transpose(3, 4, 0, 1, 2).reshape(x_block * lines_per, 2 * length)
+    columns = pencil.reshape(2 * length, x_block * lines_per)
     z_table = inverse.reshape(2, slab_count, planes, 2 * length).transpose(1, 0, 2, 3).reshape(2 * length, 2 * length)
-    z_high, z_low = halves(z_table)
+    z_high, z_low = halves(z_table.T)
+    step_x = 2
     result = pl.pallas_call(
         along_z,
         out_shape=jax.ShapeDtypeStruct((2, x_block, lines_per, length), jnp.float32),
-        grid=(x_block,),
+        grid=(x_block // step_x,),
         in_specs=[
-            pl.BlockSpec((lines_per, 2 * length), lambda i: (i, 0)),
             pl.BlockSpec((2 * length, 2 * length), lambda i: (0, 0)),
             pl.BlockSpec((2 * length, 2 * length), lambda i: (0, 0)),
+            pl.BlockSpec((2 * length, step_x * lines_per), lambda i: (0, i)),
         ],
-        out_specs=pl.BlockSpec((2, 1, lines_per, length), lambda i: (0, i, 0, 0)),
-    )(lhs, z_high, z_low)
+        out_specs=pl.BlockSpec((2, step_x, lines_per, length), lambda i: (0, i, 0, 0)),
+    )(z_high, z_low, columns)
     return result
 
 

time: 203 us -> 193 us (0.951)
  local copies, waits for them, and re-layouts: 14.2 us -> 7.76 us
  Pallas kernels: 46.4 us -> 43 us
    reshape x1 -> x0, local copies, waits for them, and re-layouts: 6.4 us -> none  [local(): pencil.transpose(3, 4, 0, 1, 2).reshape(x_block * lines_per, 2 * length)]
    pallas_call x1, Pallas kernels: 17.9 us -> 14.5 us  [local(): pl.pallas_call(along_z, out_shape=jax.ShapeDtypeStruct((2, x_block, lines...]
where the time goes in v4:
time: 193 us; the launch traced here: 192 us
  blocking collectives  124 us (64%)
  Pallas kernels  43 us (22%)
  matrix products  13.6 us (7%)
  local copies, waits for them, and re-layouts  7.76 us (4%)
  other arithmetic  2.95 us (2%)
    all_to_all x1, blocking collectives, local(): lax.all_to_all(send.reshape(devices_all, capacity, width), ('slab', 'grp'...  69.1 us
    all_to_all x1, blocking collectives, local(): lax.all_to_all(along_x, 'slab', split_axis=0, concat_axis=0, tiled=True)  55.1 us
    pallas_call x1, Pallas kernels, local(): pl.pallas_call(accumulate_and_transform, out_shape=jax.ShapeDtypeStruct((...  28.5 us
    pallas_call x1, Pallas kernels, local(): pl.pallas_call(along_z, out_shape=jax.ShapeDtypeStruct((2, x_block, lines...  14.5 us
    dot_general x1, matrix products, local(): jnp.dot(placing, payload, preferred_element_type=jnp.float32)  6.19 us
    unnamed x19, local copies, waits for them, and re-layouts  5.83 us

profile of v4, /device:TPU:0, one launch (start us, length us, event | category | flops | bytes accessed | tf_op | source)
XLA Modules:
  0.0 191.7 jit_solution(11821795079020507462)
XLA Ops:
  0.0 0.8 convert_element_type.53
  0.8 0.8 copy.16
  1.6 0.2 fusion.18
  1.9 0.1 copy.17
  2.0 0.4 fusion.17
  2.4 1.0 copy-done.4
  3.4 1.8 fusion.13
  5.3 0.0 copy-start.2
  5.3 1.9 %fusion.11 = f32[512,1024]{1,0:T(8,128)S(1)} fusion(f32[512,1024]{1,0:T(8,128)S(1)} %copy-done.3, f32[1024,512]{1,0:T(8,128)S(1)} %fusion.13), kind=kOutput, calls=%fused_computation.16 | convolution fusion | flops 1610612736 | bytes 5242880 | tf_op jit(solution)/shard_map/dot_general | solution.py:74
  7.3 2.0 %add_convert_fusion = bf16[512,1024]{1,0:T(8,128)(2,1)S(1)} fusion(f32[512,1024]{1,0:T(8,128)S(1)} %fusion.11, f32[512,1024]{1,0:T(8,128)S(1)} %copy-done.2, f32[1024,512]{1,0:T(8,128)S(1)} %fusion.13), kind=kOutput, calls=%fused_computation.8 | convolution fusion | flops 1611661312 | bytes 6291456 | tf_op jit(solution)/shard_map/dot_general | solution.py:75
  9.3 0.0 copy-start.8
  9.3 1.3 fusion.7
  10.7 0.3 fusion.9
  11.0 6.2 %fusion.1 = bf16[2048,1152]{1,0:T(8,128)(2,1)S(1)} fusion(s32[1024]{0:T(1024)S(1)} %multiply_add_fusion, bf16[1024,128]{1,0:T(8,128)(2,1)S(1)} %fusion.9, bf16[1024,1024]{1,0:T(8,128)(2,1)S(1)} %fusion.7), kind=kOutput, calls=%fused_computation.2 | convolution fusion | flops 4841013248 | bytes 7081984 | tf_op jit(solution)/shard_map/dot_general | solution.py:95
  17.2 69.1 %all_to_all.10 = bf16[128,16,1152]{2,1,0:T(8,128)(2,1)S(1)} all-to-all(bf16[128,16,1152]{2,1,0:T(8,128)(2,1)S(1)} %bitcast.46), channel_id=1, replica_groups=mesh['slab'=32,'grp'=4] {'slab','grp'}, dimensions={0} | all-to-all | bytes 9437184 | tf_op jit(solution)/shard_map/all_to_all | solution.py:97
  86.3 1.5 convert_reduce_fusion
  87.8 0.7 copy-done.1
  88.5 0.1 convert_bitcast_fusion
  88.6 0.3 copy.18
  88.9 0.7 reshape.73.weight_ref
  89.6 28.5 %shard_map.127 = bf16[32,2,16,16,128]{4,3,2,1,0:T(8,128)(2,1)} custom-call(f32[8,2,2048]{2,1,0:T(2,128)} %reshape.73.weight_ref, s32[1,2048]{1,0:T(1,128)} %bitcast.50, bf16[2048,1152]{1,0:T(8,128)(2,1)} %bitcast.43, bf16[1024,1024]{1,0:T(8,128)(2,1)} %constant.31.clone.inverse_high_ref, bf16[1024,1024]{1,0:T(8,128)(2,1)} %constant.32.clone.inverse_low_ref), custom_call_target="tpu_custom_call" | custom-call | tf_op jit(solution)/shard_map/pallas_call | solution.py:117
  118.1 55.1 %all_to_all.11 = bf16[32,2,16,16,128]{4,3,2,1,0:T(8,128)(2,1)S(1)} all-to-all(bf16[32,2,16,16,128]{4,3,2,1,0:T(8,128)(2,1)} %shard_map.127), channel_id=1, replica_groups=mesh['slab'=32,'grp'=4] {'slab'}, dimensions={0} | all-to-all | bytes 8388608 | tf_op jit(solution)/shard_map/all_to_all | solution.py:130
  173.2 4.0 %copy.21 = bf16[128,8,16,128]{3,1,2,0:T(8,128)(2,1)} copy(bf16[128,8,16,128]{3,2,1,0:T(8,128)(2,1)S(1)} %bitcast.44) | data formatting | bytes 8388608
  177.2 14.5 %shard_map.128 = f32[2,16,128,512]{3,2,1,0:T(8,128)} custom-call(bf16[1024,1024]{1,0:T(8,128)(2,1)} %constant.33.clone.z_high_ref, bf16[1024,1024]{1,0:T(8,128)(2,1)} %constant.34.clone.z_low_ref, bf16[1024,2048]{1,0:T(8,128)(2,1)} %bitcast.45), custom_call_target="tpu_custom_call" | custom-call | tf_op jit(solution)/shard_map/pallas_call | solution.py:136
  (20 shorter events, 0.1 us)
Async XLA Ops:
  0.0 2.4 %copy-start = (f32[1,512,512]{2,1,0:T(8,128)S(1)}, f32[1,512,512]{2,1,0:T(8,128)}, u32[]{:S(2)}) copy-start(f32[1,512,512]{2,1,0:T(8,128)} %param.13) | copy-start | bytes 3145732
  0.0 2.0 %copy-start.5 = (s32[1,1024,1]{1,2,0:T(1,128)S(1)}, s32[1,1024,1]{1,2,0:T(1,128)}, u32[]{:S(2)}) copy-start(s32[1,1024,1]{1,2,0:T(1,128)} %param.15) | copy-start | bytes 12292
  1.8 1.6 copy-start.4
  3.4 1.9 copy-start.3
  5.3 2.0 %copy-start.2 = (f32[512,1024]{1,0:T(8,128)S(1)}, f32[512,1024]{1,0:T(8,128)}, u32[]{:S(2)}) copy-start(f32[512,1024]{1,0:T(8,128)} %constant.29.clone) | copy-start | bytes 6291460
  7.3 2.0 %copy-start.7 = (s32[1,1024]{1,0:T(1,128)S(1)}, s32[1,1024]{1,0:T(1,128)}, u32[]{:S(2)}) copy-start(s32[1,1024]{1,0:T(1,128)} %param.14) | copy-start | bytes 12292
  9.3 1.3 copy-start.6
  9.3 1.3 copy-start.8
  86.3 2.2 %copy-start.1 = (bf16[128,16,1152]{2,1,0:T(8,128)(2,1)}, bf16[128,16,1152]{2,1,0:T(8,128)(2,1)S(1)}, u32[]{:S(2)}) copy-start(bf16[128,16,1152]{2,1,0:T(8,128)(2,1)S(1)} %all_to_all.10) | copy-start | bytes 14155780

commit v5 on v2

--- a/solution.py
+++ b/solution.py
@@ -127,8 +127,10 @@
         columns = slice(part * length, (part + 1) * length)
         flat = jnp.dot(lhs, z_high[:, columns], preferred_element_type=jnp.float32)
         flat = flat + jnp.dot(lhs, z_low[:, columns], preferred_element_type=jnp.float32)
-        parts.append(flat.reshape(x_block, lines_per, length))
-    result = jnp.stack(parts)
+        parts.append(flat.reshape(1, x_block, lines_per, length))
+    result = lax.dynamic_update_slice(
+        jnp.broadcast_to(parts[0], (2, x_block, lines_per, length)), parts[1], (1, 0, 0, 0)
+    )
     return result
 
 

time: 192 us -> 195 us (1.016)
  local copies, waits for them, and re-layouts: 2.76 us -> 10.1 us
  other arithmetic: 8.83 us -> 4.4 us
    broadcast_in_dim x0 -> x1, local copies, waits for them, and re-layouts: none -> 4.76 us  [local(): jnp.broadcast_to(parts[0], (2, x_block, lines_per, length))]
    another operation x4 -> x3, other arithmetic: 4.7 us -> 0.26 us  [the longest x1 4.43 us: local(): result = jnp.stack(parts)]
    dynamic_update_slice x0 -> x1, local copies, waits for them, and re-layouts: none -> 2.62 us  [local(): lax.dynamic_update_slice(jnp.broadcast_to(parts[0], (2, x_block, lines_pe...]
where the time goes in v5:
time: 195 us; the launch traced here: 193 us
  blocking collectives  124 us (64%)
  Pallas kernels  28.5 us (15%)
  matrix products  25.7 us (13%)
  local copies, waits for them, and re-layouts  10.1 us (5%)
  other arithmetic  4.4 us (2%)
    all_to_all x1, blocking collectives, local(): lax.all_to_all(send.reshape(devices_all, capacity, width), ('slab', 'grp'...  69.1 us
    all_to_all x1, blocking collectives, local(): lax.all_to_all(along_x, 'slab', split_axis=0, concat_axis=0, tiled=True)  55.2 us
    pallas_call x1, Pallas kernels, local(): pl.pallas_call(accumulate_and_transform, out_shape=jax.ShapeDtypeStruct((...  28.5 us
    dot_general x1, matrix products, local(): jnp.dot(placing, payload, preferred_element_type=jnp.float32)  6.19 us
    dot_general x2, matrix products, local(): flat = jnp.dot(lhs, z_high[:, columns], preferred_element_type=jnp.float32)  5.46 us
    dot_general x2, matrix products, local(): jnp.dot(lhs, z_low[:, columns], preferred_element_type=jnp.float32)  4.92 us
    broadcast_in_dim x1, local copies, waits for them, and re-layouts, local(): jnp.broadcast_to(parts[0], (2, x_block, lines_per, length))  4.76 us

profile of v5, /device:TPU:0, one launch (start us, length us, event | category | flops | bytes accessed | tf_op | source)
XLA Modules:
  0.0 193.4 jit_solution(16425424903070825706)
XLA Ops:
  0.0 0.8 convert_element_type.53
  0.8 0.8 copy.16
  1.6 0.2 fusion.36
  2.0 1.2 fusion.35
  3.2 0.7 multiply_add_fusion
  3.9 3.6 %fusion.31 = f32[1024,512]{1,0:T(8,128)S(1)} fusion(f32[1024,512]{1,0:T(8,128)} %constant.29.clone, f32[1,512,512]{2,1,0:T(8,128)S(1)} %copy-done), kind=kOutput, calls=%fused_computation.31 | convolution fusion | flops 1610612736 | bytes 5242880 | tf_op jit(solution)/shard_map/dot_general | solution.py:61
  7.4 1.9 %fusion.29 = f32[512,1024]{1,0:T(8,128)S(1)} fusion(f32[512,1024]{1,0:T(8,128)S(1)} %copy-done.4, f32[1024,512]{1,0:T(8,128)S(1)} %fusion.31), kind=kOutput, calls=%fused_computation.29 | convolution fusion | flops 1610612736 | bytes 5242880 | tf_op jit(solution)/shard_map/dot_general | solution.py:64
  9.4 2.0 %add_convert_fusion = bf16[512,1024]{1,0:T(8,128)(2,1)S(1)} fusion(f32[512,1024]{1,0:T(8,128)S(1)} %fusion.29, f32[512,1024]{1,0:T(8,128)S(1)} %copy-done.3, f32[1024,512]{1,0:T(8,128)S(1)} %fusion.31), kind=kOutput, calls=%fused_computation.21 | convolution fusion | flops 1611661312 | bytes 6291456 | tf_op jit(solution)/shard_map/dot_general | solution.py:65
  11.5 1.3 fusion.25
  12.8 0.3 fusion.27
  13.1 6.2 %fusion.1 = bf16[2048,1152]{1,0:T(8,128)(2,1)S(1)} fusion(s32[1024]{0:T(1024)S(1)} %multiply_add_fusion, bf16[1024,128]{1,0:T(8,128)(2,1)S(1)} %fusion.27, bf16[1024,1024]{1,0:T(8,128)(2,1)S(1)} %fusion.25), kind=kOutput, calls=%fused_computation.2 | convolution fusion | flops 4841013248 | bytes 7081984 | tf_op jit(solution)/shard_map/dot_general | solution.py:85
  19.3 69.1 %all_to_all.10 = bf16[128,16,1152]{2,1,0:T(8,128)(2,1)S(1)} all-to-all(bf16[128,16,1152]{2,1,0:T(8,128)(2,1)S(1)} %bitcast.63), channel_id=1, replica_groups=mesh['slab'=32,'grp'=4] {'slab','grp'}, dimensions={0} | all-to-all | bytes 9437184 | tf_op jit(solution)/shard_map/all_to_all | solution.py:87
  88.5 1.4 convert_reduce_fusion
  89.9 0.8 copy-done.2
  90.7 0.3 copy.18
  91.0 0.7 reshape.79.weight_ref
  91.8 28.5 %shard_map.127 = bf16[32,2,16,16,128]{4,3,2,1,0:T(8,128)(2,1)} custom-call(f32[8,2,2048]{2,1,0:T(2,128)} %reshape.79.weight_ref, s32[1,2048]{1,0:T(1,128)} %bitcast.73, bf16[2048,1152]{1,0:T(8,128)(2,1)} %bitcast.62, bf16[1024,1024]{1,0:T(8,128)(2,1)} %constant.33.clone.inverse_high_ref, bf16[1024,1024]{1,0:T(8,128)(2,1)} %constant.34.clone.inverse_low_ref), custom_call_target="tpu_custom_call" | custom-call | tf_op jit(solution)/shard_map/pallas_call | solution.py:107
  120.3 55.2 %all_to_all.11 = bf16[32,2,16,16,128]{4,3,2,1,0:T(8,128)(2,1)S(1)} all-to-all(bf16[32,2,16,16,128]{4,3,2,1,0:T(8,128)(2,1)} %shard_map.127), channel_id=1, replica_groups=mesh['slab'=32,'grp'=4] {'slab'}, dimensions={0} | all-to-all | bytes 8388608 | tf_op jit(solution)/shard_map/all_to_all | solution.py:120
  175.5 2.5 %fusion.2 = f32[2048,512]{1,0:T(8,128)S(1)} fusion(bf16[1024,512]{1,0:T(8,128)(2,1)S(1)} %copy-done.10, bf16[128,8,16,128]{3,2,1,0:T(8,128)(2,1)S(1)} %bitcast.65), kind=kOutput, calls=%fused_computation.3 | convolution fusion | flops 2147483648 | bytes 9437184 | tf_op jit(solution)/shard_map/dot_general | solution.py:129
  178.0 2.5 %fusion.6 = f32[2048,512]{1,0:T(8,128)S(1)} fusion(bf16[1024,512]{1,0:T(8,128)(2,1)S(1)} %copy-done.9, bf16[128,8,16,128]{3,2,1,0:T(8,128)(2,1)S(1)} %bitcast.66), kind=kOutput, calls=%fused_computation.7 | convolution fusion | flops 2147483648 | bytes 9437184 | tf_op jit(solution)/shard_map/dot_general | solution.py:129
  180.5 2.7 %fusion.14 = f32[2048,512]{1,0:T(8,128)S(1)} fusion(f32[2048,512]{1,0:T(8,128)S(1)} %fusion.2, bf16[1024,512]{1,0:T(8,128)(2,1)S(1)} %copy-done.8, bf16[128,8,16,128]{3,2,1,0:T(8,128)(2,1)S(1)} %bitcast.67), kind=kOutput, calls=%fused_computation.13 | convolution fusion | flops 2148532224 | bytes 13631488 | tf_op jit(solution)/shard_map/dot_general | solution.py:128
  183.2 2.7 %fusion.11 = f32[2048,512]{1,0:T(8,128)S(1)} fusion(f32[2048,512]{1,0:T(8,128)S(1)} %fusion.6, bf16[1024,512]{1,0:T(8,128)(2,1)S(1)} %copy-done.7, bf16[128,8,16,128]{3,2,1,0:T(8,128)(2,1)S(1)} %bitcast.68), kind=kOutput, calls=%fused_computation.12 | convolution fusion | flops 2148532224 | bytes 13631488 | tf_op jit(solution)/shard_map/dot_general | solution.py:128
  186.0 4.8 %broadcast_in_dim.36 = f32[2,16,128,512]{3,2,1,0:T(8,128)} broadcast(f32[16,128,512]{2,1,0:T(8,128)S(1)} %bitcast.64), dimensions={1,2,3} | broadcast | bytes 12582912 | tf_op jit(solution)/shard_map/broadcast_in_dim | solution.py:132
  190.8 2.6 %constant_dynamic-update-slice_fusion = f32[2,16,128,512]{3,2,1,0:T(8,128)} fusion(f32[2,16,128,512]{3,2,1,0:T(8,128)} %broadcast_in_dim.36, f32[1,16,128,512]{3,2,1,0:T(8,128)S(1)} %bitcast.69), kind=kLoop, calls=%fused_computation.48 | loop fusion | bytes 8388608 | tf_op jit(solution)/shard_map/dynamic_update_slice | solution.py:131
  (30 shorter events, 0.3 us)
Async XLA Ops:
  0.0 3.9 %copy-start = (f32[1,512,512]{2,1,0:T(8,128)S(1)}, f32[1,512,512]{2,1,0:T(8,128)}, u32[]{:S(2)}) copy-start(f32[1,512,512]{2,1,0:T(8,128)} %param.13) | copy-start | bytes 3145732
  1.8 5.6 %copy-start.4 = (f32[512,1024]{1,0:T(8,128)S(1)}, f32[512,1024]{1,0:T(8,128)}, u32[]{:S(2)}) copy-start(f32[512,1024]{1,0:T(8,128)} %constant.30.clone) | copy-start | bytes 6291460
  3.9 5.5 %copy-start.3 = (f32[512,1024]{1,0:T(8,128)S(1)}, f32[512,1024]{1,0:T(8,128)}, u32[]{:S(2)}) copy-start(f32[512,1024]{1,0:T(8,128)} %constant.31.clone) | copy-start | bytes 6291460
  9.4 2.0 %copy-start.6 = (s32[1,1024]{1,0:T(1,128)S(1)}, s32[1,1024]{1,0:T(1,128)}, u32[]{:S(2)}) copy-start(s32[1,1024]{1,0:T(1,128)} %param.14) | copy-start | bytes 12292
  11.5 1.3 copy-start.5
  11.5 1.3 copy-start.11
  88.5 2.2 %copy-start.2 = (bf16[128,16,1152]{2,1,0:T(8,128)(2,1)}, bf16[128,16,1152]{2,1,0:T(8,128)(2,1)S(1)}, u32[]{:S(2)}) copy-start(bf16[128,16,1152]{2,1,0:T(8,128)(2,1)S(1)} %all_to_all.10) | copy-start | bytes 14155780
  120.3 55.2 %copy-start.10 = (bf16[1024,512]{1,0:T(8,128)(2,1)S(1)}, bf16[1024,512]{1,0:T(8,128)(2,1)}, u32[]{:S(2)}) copy-start(bf16[1024,512]{1,0:T(8,128)(2,1)} %constant.45) | copy-start | bytes 3145732
  175.5 2.5 %copy-start.9 = (bf16[1024,512]{1,0:T(8,128)(2,1)S(1)}, bf16[1024,512]{1,0:T(8,128)(2,1)}, u32[]{:S(2)}) copy-start(bf16[1024,512]{1,0:T(8,128)(2,1)} %constant.43) | copy-start | bytes 3145732
  178.0 2.5 %copy-start.8 = (bf16[1024,512]{1,0:T(8,128)(2,1)S(1)}, bf16[1024,512]{1,0:T(8,128)(2,1)}, u32[]{:S(2)}) copy-start(bf16[1024,512]{1,0:T(8,128)(2,1)} %constant.44) | copy-start | bytes 3145732
  180.5 2.8 %copy-start.7 = (bf16[1024,512]{1,0:T(8,128)(2,1)S(1)}, bf16[1024,512]{1,0:T(8,128)(2,1)}, u32[]{:S(2)}) copy-start(bf16[1024,512]{1,0:T(8,128)(2,1)} %constant.42) | copy-start | bytes 3145732
  186.0 7.4 %copy-start.1 = (f32[1,512,512]{2,1,0:T(8,128)S(1)}, f32[1,512,512]{2,1,0:T(8,128)}, u32[]{:S(2)}) copy-start(f32[1,512,512]{2,1,0:T(8,128)} %param.13) | copy-start | bytes 3145732

commit v6 on v2

--- a/solution.py
+++ b/solution.py
@@ -88,7 +88,7 @@
         send.reshape(devices_all, capacity, width), ("slab", "grp"), split_axis=0, concat_axis=0, tiled=True
     ).reshape(slot_count, width)
 
-    step_planes = 2
+    step_planes = 4
     weight_in = (
         got[:, 2 * length : 2 * length + planes].T.astype(jnp.float32).reshape(planes // step_planes, step_planes, slot_count)
     )

time: 192 us -> 190 us (0.990)
  no operation moved by 1% of the time
where the time goes in v6:
time: 190 us; the launch traced here: 189 us
  blocking collectives  124 us (65%)
  Pallas kernels  26.9 us (14%)
  matrix products  26 us (14%)
  other arithmetic  8.83 us (5%)
  local copies, waits for them, and re-layouts  2.72 us (1%)
    all_to_all x1, blocking collectives, local(): lax.all_to_all(send.reshape(devices_all, capacity, width), ('slab', 'grp'...  69.1 us
    all_to_all x1, blocking collectives, local(): lax.all_to_all(along_x, 'slab', split_axis=0, concat_axis=0, tiled=True)  55.2 us
    pallas_call x1, Pallas kernels, local(): pl.pallas_call(accumulate_and_transform, out_shape=jax.ShapeDtypeStruct((...  26.9 us
    dot_general x1, matrix products, local(): jnp.dot(placing, payload, preferred_element_type=jnp.float32)  6.19 us
    dot_general x2, matrix products, local(): flat = jnp.dot(lhs, z_high[:, columns], preferred_element_type=jnp.float32)  5.79 us
    dot_general x2, matrix products, local(): jnp.dot(lhs, z_low[:, columns], preferred_element_type=jnp.float32)  4.91 us
    another operation x1, other arithmetic, local(): result = jnp.stack(parts)  4.43 us

profile of v6, /device:TPU:0, one launch (start us, length us, event | category | flops | bytes accessed | tf_op | source)
XLA Modules:
  0.0 189.1 jit_solution(9676676287926563626)
XLA Ops:
  0.0 0.8 convert_element_type.53
  0.8 0.8 copy.16
  1.6 0.2 fusion.36
  1.9 0.1 copy.17
  2.0 1.2 fusion.35
  3.2 0.7 multiply_add_fusion
  3.9 3.6 %fusion.31 = f32[1024,512]{1,0:T(8,128)S(1)} fusion(f32[1024,512]{1,0:T(8,128)} %constant.27.clone, f32[1,512,512]{2,1,0:T(8,128)S(1)} %copy-done), kind=kOutput, calls=%fused_computation.32 | convolution fusion | flops 1610612736 | bytes 5242880 | tf_op jit(solution)/shard_map/dot_general | solution.py:61
  7.4 1.9 %fusion.29 = f32[512,1024]{1,0:T(8,128)S(1)} fusion(f32[512,1024]{1,0:T(8,128)S(1)} %copy-done.4, f32[1024,512]{1,0:T(8,128)S(1)} %fusion.31), kind=kOutput, calls=%fused_computation.30 | convolution fusion | flops 1610612736 | bytes 5242880 | tf_op jit(solution)/shard_map/dot_general | solution.py:64
  9.4 2.0 %add_convert_fusion = bf16[512,1024]{1,0:T(8,128)(2,1)S(1)} fusion(f32[512,1024]{1,0:T(8,128)S(1)} %fusion.29, f32[512,1024]{1,0:T(8,128)S(1)} %copy-done.3, f32[1024,512]{1,0:T(8,128)S(1)} %fusion.31), kind=kOutput, calls=%fused_computation.22 | convolution fusion | flops 1611661312 | bytes 6291456 | tf_op jit(solution)/shard_map/dot_general | solution.py:65
  11.5 1.3 fusion.25
  12.8 0.3 fusion.27
  13.1 6.2 %fusion.1 = bf16[2048,1152]{1,0:T(8,128)(2,1)S(1)} fusion(s32[1024]{0:T(1024)S(1)} %multiply_add_fusion, bf16[1024,128]{1,0:T(8,128)(2,1)S(1)} %fusion.27, bf16[1024,1024]{1,0:T(8,128)(2,1)S(1)} %fusion.25), kind=kOutput, calls=%fused_computation.3 | convolution fusion | flops 4841013248 | bytes 7081984 | tf_op jit(solution)/shard_map/dot_general | solution.py:85
  19.3 69.1 %all_to_all.10 = bf16[128,16,1152]{2,1,0:T(8,128)(2,1)S(1)} all-to-all(bf16[128,16,1152]{2,1,0:T(8,128)(2,1)S(1)} %bitcast.63), channel_id=1, replica_groups=mesh['slab'=32,'grp'=4] {'slab','grp'}, dimensions={0} | all-to-all | bytes 9437184 | tf_op jit(solution)/shard_map/all_to_all | solution.py:87
  88.5 1.4 convert_reduce_fusion
  89.9 0.8 copy-done.2
  90.7 0.3 copy.18
  91.0 0.7 reshape.73.weight_ref
  91.7 26.9 %shard_map.127 = bf16[32,2,16,16,128]{4,3,2,1,0:T(8,128)(2,1)} custom-call(f32[4,4,2048]{2,1,0:T(4,128)} %reshape.73.weight_ref, s32[1,2048]{1,0:T(1,128)} %bitcast.73, bf16[2048,1152]{1,0:T(8,128)(2,1)} %bitcast.62, bf16[1024,1024]{1,0:T(8,128)(2,1)} %constant.31.clone.inverse_high_ref, bf16[1024,1024]{1,0:T(8,128)(2,1)} %constant.32.clone.inverse_low_ref), custom_call_target="tpu_custom_call" | custom-call | tf_op jit(solution)/shard_map/pallas_call | solution.py:107
  118.6 55.2 %all_to_all.11 = bf16[32,2,16,16,128]{4,3,2,1,0:T(8,128)(2,1)S(1)} all-to-all(bf16[32,2,16,16,128]{4,3,2,1,0:T(8,128)(2,1)} %shard_map.127), channel_id=1, replica_groups=mesh['slab'=32,'grp'=4] {'slab'}, dimensions={0} | all-to-all | bytes 8388608 | tf_op jit(solution)/shard_map/all_to_all | solution.py:120
  173.9 2.5 %fusion.2 = f32[2048,512]{1,0:T(8,128)S(1)} fusion(bf16[1024,512]{1,0:T(8,128)(2,1)S(1)} %copy-done.10, bf16[128,8,16,128]{3,2,1,0:T(8,128)(2,1)S(1)} %bitcast.64), kind=kOutput, calls=%fused_computation.4 | convolution fusion | flops 2147483648 | bytes 9437184 | tf_op jit(solution)/shard_map/dot_general | solution.py:129
  176.4 2.5 %fusion.6 = f32[2048,512]{1,0:T(8,128)S(1)} fusion(bf16[1024,512]{1,0:T(8,128)(2,1)S(1)} %copy-done.9, bf16[128,8,16,128]{3,2,1,0:T(8,128)(2,1)S(1)} %bitcast.65), kind=kOutput, calls=%fused_computation.8 | convolution fusion | flops 2147483648 | bytes 9437184 | tf_op jit(solution)/shard_map/dot_general | solution.py:129
  178.9 2.9 %fusion.14 = f32[2048,512]{1,0:T(8,128)S(1)} fusion(f32[2048,512]{1,0:T(8,128)S(1)} %fusion.2, bf16[1024,512]{1,0:T(8,128)(2,1)S(1)} %copy-done.8, bf16[128,8,16,128]{3,2,1,0:T(8,128)(2,1)S(1)} %bitcast.66), kind=kOutput, calls=%fused_computation.14 | convolution fusion | flops 2148532224 | bytes 13631488 | tf_op jit(solution)/shard_map/dot_general | solution.py:128
  181.8 2.9 %fusion.11 = f32[2048,512]{1,0:T(8,128)S(1)} fusion(f32[2048,512]{1,0:T(8,128)S(1)} %fusion.6, bf16[1024,512]{1,0:T(8,128)(2,1)S(1)} %copy-done.7, bf16[128,8,16,128]{3,2,1,0:T(8,128)(2,1)S(1)} %bitcast.67), kind=kOutput, calls=%fused_computation.13 | convolution fusion | flops 2148532224 | bytes 13631488 | tf_op jit(solution)/shard_map/dot_general | solution.py:128
  184.7 4.4 %pad_maximum_fusion = f32[2,16,128,512]{3,2,1,0:T(8,128)} fusion(f32[1,16,128,512]{3,2,1,0:T(8,128)S(1)} %bitcast.68, f32[1,16,128,512]{3,2,1,0:T(8,128)S(1)} %bitcast.69), kind=kLoop, calls=%fused_computation | loop fusion | flops 2097152 | bytes 16777216 | tf_op jit(solution)/shard_map/stack | solution.py:131
  (29 shorter events, 0.2 us)
Async XLA Ops:
  0.0 3.9 %copy-start = (f32[1,512,512]{2,1,0:T(8,128)S(1)}, f32[1,512,512]{2,1,0:T(8,128)}, u32[]{:S(2)}) copy-start(f32[1,512,512]{2,1,0:T(8,128)} %param.13) | copy-start | bytes 3145732
  1.8 5.6 %copy-start.4 = (f32[512,1024]{1,0:T(8,128)S(1)}, f32[512,1024]{1,0:T(8,128)}, u32[]{:S(2)}) copy-start(f32[512,1024]{1,0:T(8,128)} %constant.28.clone) | copy-start | bytes 6291460
  3.9 5.5 %copy-start.3 = (f32[512,1024]{1,0:T(8,128)S(1)}, f32[512,1024]{1,0:T(8,128)}, u32[]{:S(2)}) copy-start(f32[512,1024]{1,0:T(8,128)} %constant.29.clone) | copy-start | bytes 6291460
  9.4 2.0 %copy-start.6 = (s32[1,1024]{1,0:T(1,128)S(1)}, s32[1,1024]{1,0:T(1,128)}, u32[]{:S(2)}) copy-start(s32[1,1024]{1,0:T(1,128)} %param.14) | copy-start | bytes 12292
  11.5 1.3 copy-start.5
  11.5 1.3 copy-start.11
  88.5 2.2 %copy-start.2 = (bf16[128,16,1152]{2,1,0:T(8,128)(2,1)}, bf16[128,16,1152]{2,1,0:T(8,128)(2,1)S(1)}, u32[]{:S(2)}) copy-start(bf16[128,16,1152]{2,1,0:T(8,128)(2,1)S(1)} %all_to_all.10) | copy-start | bytes 14155780
  118.6 55.2 %copy-start.10 = (bf16[1024,512]{1,0:T(8,128)(2,1)S(1)}, bf16[1024,512]{1,0:T(8,128)(2,1)}, u32[]{:S(2)}) copy-start(bf16[1024,512]{1,0:T(8,128)(2,1)} %constant.43) | copy-start | bytes 3145732
  173.9 2.5 %copy-start.9 = (bf16[1024,512]{1,0:T(8,128)(2,1)S(1)}, bf16[1024,512]{1,0:T(8,128)(2,1)}, u32[]{:S(2)}) copy-start(bf16[1024,512]{1,0:T(8,128)(2,1)} %constant.41) | copy-start | bytes 3145732
  176.4 2.5 %copy-start.8 = (bf16[1024,512]{1,0:T(8,128)(2,1)S(1)}, bf16[1024,512]{1,0:T(8,128)(2,1)}, u32[]{:S(2)}) copy-start(bf16[1024,512]{1,0:T(8,128)(2,1)} %constant.42) | copy-start | bytes 3145732
  178.8 2.9 %copy-start.7 = (bf16[1024,512]{1,0:T(8,128)(2,1)S(1)}, bf16[1024,512]{1,0:T(8,128)(2,1)}, u32[]{:S(2)}) copy-start(bf16[1024,512]{1,0:T(8,128)(2,1)} %constant.40) | copy-start | bytes 3145732
  184.7 4.4 %copy-start.1 = (f32[1,512,512]{2,1,0:T(8,128)S(1)}, f32[1,512,512]{2,1,0:T(8,128)}, u32[]{:S(2)}) copy-start(f32[1,512,512]{2,1,0:T(8,128)} %param.13) | copy-start | bytes 3145732

commit v7 on v6

--- a/solution.py
+++ b/solution.py
@@ -88,7 +88,7 @@
         send.reshape(devices_all, capacity, width), ("slab", "grp"), split_axis=0, concat_axis=0, tiled=True
     ).reshape(slot_count, width)
 
-    step_planes = 4
+    step_planes = 8
     weight_in = (
         got[:, 2 * length : 2 * length + planes].T.astype(jnp.float32).reshape(planes // step_planes, step_planes, slot_count)
     )

time: 190 us -> 190 us (level)
  no operation moved by 1% of the time
where the time goes in v7:
time: 190 us; the launch traced here: 189 us
  blocking collectives  124 us (65%)
  Pallas kernels  27 us (14%)
  matrix products  26 us (14%)
  other arithmetic  8.83 us (5%)
  local copies, waits for them, and re-layouts  2.68 us (1%)
    all_to_all x1, blocking collectives, local(): lax.all_to_all(send.reshape(devices_all, capacity, width), ('slab', 'grp'...  69.1 us
    all_to_all x1, blocking collectives, local(): lax.all_to_all(along_x, 'slab', split_axis=0, concat_axis=0, tiled=True)  55.2 us
    pallas_call x1, Pallas kernels, local(): pl.pallas_call(accumulate_and_transform, out_shape=jax.ShapeDtypeStruct((...  27 us
    dot_general x1, matrix products, local(): jnp.dot(placing, payload, preferred_element_type=jnp.float32)  6.19 us
    dot_general x2, matrix products, local(): flat = jnp.dot(lhs, z_high[:, columns], preferred_element_type=jnp.float32)  5.79 us
    dot_general x2, matrix products, local(): jnp.dot(lhs, z_low[:, columns], preferred_element_type=jnp.float32)  4.92 us
    another operation x1, other arithmetic, local(): result = jnp.stack(parts)  4.43 us

profile of v7, /device:TPU:0, one launch (start us, length us, event | category | flops | bytes accessed | tf_op | source)
XLA Modules:
  0.0 189.1 jit_solution(7501793897086208819)
XLA Ops:
  0.0 0.8 convert_element_type.53
  0.8 0.8 copy.16
  1.6 0.2 fusion.36
  1.9 0.1 copy.17
  2.0 1.2 fusion.35
  3.2 0.7 multiply_add_fusion
  3.9 3.6 %fusion.31 = f32[1024,512]{1,0:T(8,128)S(1)} fusion(f32[1024,512]{1,0:T(8,128)} %constant.27.clone, f32[1,512,512]{2,1,0:T(8,128)S(1)} %copy-done), kind=kOutput, calls=%fused_computation.32 | convolution fusion | flops 1610612736 | bytes 5242880 | tf_op jit(solution)/shard_map/dot_general | solution.py:61
  7.4 1.9 %fusion.29 = f32[512,1024]{1,0:T(8,128)S(1)} fusion(f32[512,1024]{1,0:T(8,128)S(1)} %copy-done.4, f32[1024,512]{1,0:T(8,128)S(1)} %fusion.31), kind=kOutput, calls=%fused_computation.30 | convolution fusion | flops 1610612736 | bytes 5242880 | tf_op jit(solution)/shard_map/dot_general | solution.py:64
  9.4 2.0 %add_convert_fusion = bf16[512,1024]{1,0:T(8,128)(2,1)S(1)} fusion(f32[512,1024]{1,0:T(8,128)S(1)} %fusion.29, f32[512,1024]{1,0:T(8,128)S(1)} %copy-done.3, f32[1024,512]{1,0:T(8,128)S(1)} %fusion.31), kind=kOutput, calls=%fused_computation.22 | convolution fusion | flops 1611661312 | bytes 6291456 | tf_op jit(solution)/shard_map/dot_general | solution.py:65
  11.5 1.3 fusion.25
  12.8 0.3 fusion.27
  13.1 6.2 %fusion.1 = bf16[2048,1152]{1,0:T(8,128)(2,1)S(1)} fusion(s32[1024]{0:T(1024)S(1)} %multiply_add_fusion, bf16[1024,128]{1,0:T(8,128)(2,1)S(1)} %fusion.27, bf16[1024,1024]{1,0:T(8,128)(2,1)S(1)} %fusion.25), kind=kOutput, calls=%fused_computation.3 | convolution fusion | flops 4841013248 | bytes 7081984 | tf_op jit(solution)/shard_map/dot_general | solution.py:85
  19.3 69.1 %all_to_all.10 = bf16[128,16,1152]{2,1,0:T(8,128)(2,1)S(1)} all-to-all(bf16[128,16,1152]{2,1,0:T(8,128)(2,1)S(1)} %bitcast.64), channel_id=1, replica_groups=mesh['slab'=32,'grp'=4] {'slab','grp'}, dimensions={0} | all-to-all | bytes 9437184 | tf_op jit(solution)/shard_map/all_to_all | solution.py:87
  88.5 1.4 convert_reduce_fusion
  89.9 0.8 copy-done.2
  90.6 0.1 convert_bitcast_fusion
  90.7 1.0 copy.18
  91.7 27.0 %shard_map.127 = bf16[32,2,16,16,128]{4,3,2,1,0:T(8,128)(2,1)} custom-call(f32[2,8,2048]{2,1,0:T(8,128)} %bitcast.71, s32[1,2048]{1,0:T(1,128)} %bitcast.75, bf16[2048,1152]{1,0:T(8,128)(2,1)} %bitcast.63, bf16[1024,1024]{1,0:T(8,128)(2,1)} %constant.31.clone.inverse_high_ref, bf16[1024,1024]{1,0:T(8,128)(2,1)} %constant.32.clone.inverse_low_ref), custom_call_target="tpu_custom_call" | custom-call | tf_op jit(solution)/shard_map/pallas_call | solution.py:107
  118.6 55.2 %all_to_all.11 = bf16[32,2,16,16,128]{4,3,2,1,0:T(8,128)(2,1)S(1)} all-to-all(bf16[32,2,16,16,128]{4,3,2,1,0:T(8,128)(2,1)} %shard_map.127), channel_id=1, replica_groups=mesh['slab'=32,'grp'=4] {'slab'}, dimensions={0} | all-to-all | bytes 8388608 | tf_op jit(solution)/shard_map/all_to_all | solution.py:120
  173.9 2.5 %fusion.2 = f32[2048,512]{1,0:T(8,128)S(1)} fusion(bf16[1024,512]{1,0:T(8,128)(2,1)S(1)} %copy-done.10, bf16[128,8,16,128]{3,2,1,0:T(8,128)(2,1)S(1)} %bitcast.65), kind=kOutput, calls=%fused_computation.4 | convolution fusion | flops 2147483648 | bytes 9437184 | tf_op jit(solution)/shard_map/dot_general | solution.py:129
  176.4 2.5 %fusion.6 = f32[2048,512]{1,0:T(8,128)S(1)} fusion(bf16[1024,512]{1,0:T(8,128)(2,1)S(1)} %copy-done.9, bf16[128,8,16,128]{3,2,1,0:T(8,128)(2,1)S(1)} %bitcast.66), kind=kOutput, calls=%fused_computation.8 | convolution fusion | flops 2147483648 | bytes 9437184 | tf_op jit(solution)/shard_map/dot_general | solution.py:129
  178.9 2.9 %fusion.14 = f32[2048,512]{1,0:T(8,128)S(1)} fusion(f32[2048,512]{1,0:T(8,128)S(1)} %fusion.2, bf16[1024,512]{1,0:T(8,128)(2,1)S(1)} %copy-done.8, bf16[128,8,16,128]{3,2,1,0:T(8,128)(2,1)S(1)} %bitcast.67), kind=kOutput, calls=%fused_computation.14 | convolution fusion | flops 2148532224 | bytes 13631488 | tf_op jit(solution)/shard_map/dot_general | solution.py:128
  181.8 2.9 %fusion.11 = f32[2048,512]{1,0:T(8,128)S(1)} fusion(f32[2048,512]{1,0:T(8,128)S(1)} %fusion.6, bf16[1024,512]{1,0:T(8,128)(2,1)S(1)} %copy-done.7, bf16[128,8,16,128]{3,2,1,0:T(8,128)(2,1)S(1)} %bitcast.68), kind=kOutput, calls=%fused_computation.13 | convolution fusion | flops 2148532224 | bytes 13631488 | tf_op jit(solution)/shard_map/dot_general | solution.py:128
  184.7 4.4 %pad_maximum_fusion = f32[2,16,128,512]{3,2,1,0:T(8,128)} fusion(f32[1,16,128,512]{3,2,1,0:T(8,128)S(1)} %bitcast.69, f32[1,16,128,512]{3,2,1,0:T(8,128)S(1)} %bitcast.70), kind=kLoop, calls=%fused_computation | loop fusion | flops 2097152 | bytes 16777216 | tf_op jit(solution)/shard_map/stack | solution.py:131
  (28 shorter events, 0.1 us)
Async XLA Ops:
  0.0 3.9 %copy-start = (f32[1,512,512]{2,1,0:T(8,128)S(1)}, f32[1,512,512]{2,1,0:T(8,128)}, u32[]{:S(2)}) copy-start(f32[1,512,512]{2,1,0:T(8,128)} %param.13) | copy-start | bytes 3145732
  1.8 5.6 %copy-start.4 = (f32[512,1024]{1,0:T(8,128)S(1)}, f32[512,1024]{1,0:T(8,128)}, u32[]{:S(2)}) copy-start(f32[512,1024]{1,0:T(8,128)} %constant.28.clone) | copy-start | bytes 6291460
  3.9 5.5 %copy-start.3 = (f32[512,1024]{1,0:T(8,128)S(1)}, f32[512,1024]{1,0:T(8,128)}, u32[]{:S(2)}) copy-start(f32[512,1024]{1,0:T(8,128)} %constant.29.clone) | copy-start | bytes 6291460
  9.4 2.0 %copy-start.6 = (s32[1,1024]{1,0:T(1,128)S(1)}, s32[1,1024]{1,0:T(1,128)}, u32[]{:S(2)}) copy-start(s32[1,1024]{1,0:T(1,128)} %param.14) | copy-start | bytes 12292
  11.5 1.3 copy-start.5
  11.5 1.3 copy-start.11
  88.5 2.2 %copy-start.2 = (bf16[128,16,1152]{2,1,0:T(8,128)(2,1)}, bf16[128,16,1152]{2,1,0:T(8,128)(2,1)S(1)}, u32[]{:S(2)}) copy-start(bf16[128,16,1152]{2,1,0:T(8,128)(2,1)S(1)} %all_to_all.10) | copy-start | bytes 14155780
  118.6 55.2 %copy-start.10 = (bf16[1024,512]{1,0:T(8,128)(2,1)S(1)}, bf16[1024,512]{1,0:T(8,128)(2,1)}, u32[]{:S(2)}) copy-start(bf16[1024,512]{1,0:T(8,128)(2,1)} %constant.43) | copy-start | bytes 3145732
  173.9 2.5 %copy-start.9 = (bf16[1024,512]{1,0:T(8,128)(2,1)S(1)}, bf16[1024,512]{1,0:T(8,128)(2,1)}, u32[]{:S(2)}) copy-start(bf16[1024,512]{1,0:T(8,128)(2,1)} %constant.41) | copy-start | bytes 3145732
  176.4 2.5 %copy-start.8 = (bf16[1024,512]{1,0:T(8,128)(2,1)S(1)}, bf16[1024,512]{1,0:T(8,128)(2,1)}, u32[]{:S(2)}) copy-start(bf16[1024,512]{1,0:T(8,128)(2,1)} %constant.42) | copy-start | bytes 3145732
  178.8 2.9 %copy-start.7 = (bf16[1024,512]{1,0:T(8,128)(2,1)S(1)}, bf16[1024,512]{1,0:T(8,128)(2,1)}, u32[]{:S(2)}) copy-start(bf16[1024,512]{1,0:T(8,128)(2,1)} %constant.40) | copy-start | bytes 3145732
  184.7 4.4 %copy-start.1 = (f32[1,512,512]{2,1,0:T(8,128)S(1)}, f32[1,512,512]{2,1,0:T(8,128)}, u32[]{:S(2)}) copy-start(f32[1,512,512]{2,1,0:T(8,128)} %param.13) | copy-start | bytes 3145732

commit v8 on v7

--- a/solution.py
+++ b/solution.py
@@ -88,7 +88,7 @@
         send.reshape(devices_all, capacity, width), ("slab", "grp"), split_axis=0, concat_axis=0, tiled=True
     ).reshape(slot_count, width)
 
-    step_planes = 8
+    step_planes = 16
     weight_in = (
         got[:, 2 * length : 2 * length + planes].T.astype(jnp.float32).reshape(planes // step_planes, step_planes, slot_count)
     )

time: 190 us -> 205 us (1.079)
  the two profiles are of different devices: /device:TPU:0 before, /device:TPU:1 now
where the time goes in v8:
time: 205 us; the launch traced here: 201 us
  blocking collectives  125 us (61%)
  Pallas kernels  38.1 us (19%)
  matrix products  26 us (13%)
  other arithmetic  8.83 us (4%)
  local copies, waits for them, and re-layouts  2.68 us (1%)
    all_to_all x1, blocking collectives, local(): lax.all_to_all(send.reshape(devices_all, capacity, width), ('slab', 'grp'...  70 us
    all_to_all x1, blocking collectives, local(): lax.all_to_all(along_x, 'slab', split_axis=0, concat_axis=0, tiled=True)  55.4 us
    pallas_call x1, Pallas kernels, local(): pl.pallas_call(accumulate_and_transform, out_shape=jax.ShapeDtypeStruct((...  38.1 us
    dot_general x1, matrix products, local(): jnp.dot(placing, payload, preferred_element_type=jnp.float32)  6.19 us
    dot_general x2, matrix products, local(): flat = jnp.dot(lhs, z_high[:, columns], preferred_element_type=jnp.float32)  5.79 us
    dot_general x2, matrix products, local(): jnp.dot(lhs, z_low[:, columns], preferred_element_type=jnp.float32)  4.91 us
    another operation x1, other arithmetic, local(): result = jnp.stack(parts)  4.43 us

profile of v8, /device:TPU:1, one launch (start us, length us, event | category | flops | bytes accessed | tf_op | source)
XLA Modules:
  0.0 201.5 jit_solution(3186077646195283789)
XLA Ops:
  0.0 0.8 convert_element_type.53
  0.8 0.8 copy.16
  1.6 0.2 fusion.36
  1.9 0.1 copy.17
  2.0 1.2 fusion.35
  3.2 0.7 multiply_add_fusion
  3.9 3.6 %fusion.31 = f32[1024,512]{1,0:T(8,128)S(1)} fusion(f32[1024,512]{1,0:T(8,128)} %constant.27.clone, f32[1,512,512]{2,1,0:T(8,128)S(1)} %copy-done), kind=kOutput, calls=%fused_computation.32 | convolution fusion | flops 1610612736 | bytes 5242880 | tf_op jit(solution)/shard_map/dot_general | solution.py:61
  7.4 1.9 fusion.29
  9.4 2.0 %add_convert_fusion = bf16[512,1024]{1,0:T(8,128)(2,1)S(1)} fusion(f32[512,1024]{1,0:T(8,128)S(1)} %fusion.29, f32[512,1024]{1,0:T(8,128)S(1)} %copy-done.3, f32[1024,512]{1,0:T(8,128)S(1)} %fusion.31), kind=kOutput, calls=%fused_computation.22 | convolution fusion | flops 1611661312 | bytes 6291456 | tf_op jit(solution)/shard_map/dot_general | solution.py:65
  11.5 1.3 fusion.25
  12.8 0.3 fusion.27
  13.1 6.2 %fusion.1 = bf16[2048,1152]{1,0:T(8,128)(2,1)S(1)} fusion(s32[1024]{0:T(1024)S(1)} %multiply_add_fusion, bf16[1024,128]{1,0:T(8,128)(2,1)S(1)} %fusion.27, bf16[1024,1024]{1,0:T(8,128)(2,1)S(1)} %fusion.25), kind=kOutput, calls=%fused_computation.3 | convolution fusion | flops 4841013248 | bytes 7081984 | tf_op jit(solution)/shard_map/dot_general | solution.py:85
  19.3 70.0 %all_to_all.10 = bf16[128,16,1152]{2,1,0:T(8,128)(2,1)S(1)} all-to-all(bf16[128,16,1152]{2,1,0:T(8,128)(2,1)S(1)} %bitcast.65), channel_id=1, replica_groups=mesh['slab'=32,'grp'=4] {'slab','grp'}, dimensions={0} | all-to-all | bytes 9437184 | tf_op jit(solution)/shard_map/all_to_all | solution.py:87
  89.3 1.4 convert_reduce_fusion
  90.7 0.8 copy-done.2
  91.5 0.1 convert_bitcast_fusion
  91.6 1.0 copy.18.weight_ref
  92.5 38.1 %shard_map.127 = bf16[32,2,16,16,128]{4,3,2,1,0:T(8,128)(2,1)} custom-call(f32[1,16,2048]{2,1,0:T(8,128)} %copy.18.weight_ref, s32[1,2048]{1,0:T(1,128)} %bitcast.75, bf16[2048,1152]{1,0:T(8,128)(2,1)} %bitcast.64, bf16[1024,1024]{1,0:T(8,128)(2,1)} %constant.31.clone.inverse_high_ref, bf16[1024,1024]{1,0:T(8,128)(2,1)} %constant.32.clone.inverse_low_ref), custom_call_target="tpu_custom_call" | custom-call | tf_op jit(solution)/shard_map/pallas_call | solution.py:107
  130.6 55.4 %all_to_all.11 = bf16[32,2,16,16,128]{4,3,2,1,0:T(8,128)(2,1)S(1)} all-to-all(bf16[32,2,16,16,128]{4,3,2,1,0:T(8,128)(2,1)} %shard_map.127), channel_id=1, replica_groups=mesh['slab'=32,'grp'=4] {'slab'}, dimensions={0} | all-to-all | bytes 8388608 | tf_op jit(solution)/shard_map/all_to_all | solution.py:120
  186.1 2.5 %fusion.2 = f32[2048,512]{1,0:T(8,128)S(1)} fusion(bf16[1024,512]{1,0:T(8,128)(2,1)S(1)} %copy-done.10, bf16[128,8,16,128]{3,2,1,0:T(8,128)(2,1)S(1)} %bitcast.66), kind=kOutput, calls=%fused_computation.4 | convolution fusion | flops 2147483648 | bytes 9437184 | tf_op jit(solution)/shard_map/dot_general | solution.py:129
  188.5 2.5 %fusion.6 = f32[2048,512]{1,0:T(8,128)S(1)} fusion(bf16[1024,512]{1,0:T(8,128)(2,1)S(1)} %copy-done.9, bf16[128,8,16,128]{3,2,1,0:T(8,128)(2,1)S(1)} %bitcast.67), kind=kOutput, calls=%fused_computation.8 | convolution fusion | flops 2147483648 | bytes 9437184 | tf_op jit(solution)/shard_map/dot_general | solution.py:129
  191.0 2.9 %fusion.14 = f32[2048,512]{1,0:T(8,128)S(1)} fusion(f32[2048,512]{1,0:T(8,128)S(1)} %fusion.2, bf16[1024,512]{1,0:T(8,128)(2,1)S(1)} %copy-done.8, bf16[128,8,16,128]{3,2,1,0:T(8,128)(2,1)S(1)} %bitcast.68), kind=kOutput, calls=%fused_computation.14 | convolution fusion | flops 2148532224 | bytes 13631488 | tf_op jit(solution)/shard_map/dot_general | solution.py:128
  193.9 2.9 %fusion.11 = f32[2048,512]{1,0:T(8,128)S(1)} fusion(f32[2048,512]{1,0:T(8,128)S(1)} %fusion.6, bf16[1024,512]{1,0:T(8,128)(2,1)S(1)} %copy-done.7, bf16[128,8,16,128]{3,2,1,0:T(8,128)(2,1)S(1)} %bitcast.69), kind=kOutput, calls=%fused_computation.13 | convolution fusion | flops 2148532224 | bytes 13631488 | tf_op jit(solution)/shard_map/dot_general | solution.py:128
  196.9 4.4 %pad_maximum_fusion = f32[2,16,128,512]{3,2,1,0:T(8,128)} fusion(f32[1,16,128,512]{3,2,1,0:T(8,128)S(1)} %bitcast.70, f32[1,16,128,512]{3,2,1,0:T(8,128)S(1)} %bitcast.71), kind=kLoop, calls=%fused_computation | loop fusion | flops 2097152 | bytes 16777216 | tf_op jit(solution)/shard_map/stack | solution.py:131
  (28 shorter events, 0.1 us)
Async XLA Ops:
  0.0 3.9 %copy-start = (f32[1,512,512]{2,1,0:T(8,128)S(1)}, f32[1,512,512]{2,1,0:T(8,128)}, u32[]{:S(2)}) copy-start(f32[1,512,512]{2,1,0:T(8,128)} %param.13) | copy-start | bytes 3145732
  1.8 5.6 %copy-start.4 = (f32[512,1024]{1,0:T(8,128)S(1)}, f32[512,1024]{1,0:T(8,128)}, u32[]{:S(2)}) copy-start(f32[512,1024]{1,0:T(8,128)} %constant.28.clone) | copy-start | bytes 6291460
  3.9 5.5 %copy-start.3 = (f32[512,1024]{1,0:T(8,128)S(1)}, f32[512,1024]{1,0:T(8,128)}, u32[]{:S(2)}) copy-start(f32[512,1024]{1,0:T(8,128)} %constant.29.clone) | copy-start | bytes 6291460
  9.4 2.0 %copy-start.6 = (s32[1,1024]{1,0:T(1,128)S(1)}, s32[1,1024]{1,0:T(1,128)}, u32[]{:S(2)}) copy-start(s32[1,1024]{1,0:T(1,128)} %param.14) | copy-start | bytes 12292
  11.5 1.3 copy-start.5
  11.5 1.3 copy-start.11
  89.3 2.2 %copy-start.2 = (bf16[128,16,1152]{2,1,0:T(8,128)(2,1)}, bf16[128,16,1152]{2,1,0:T(8,128)(2,1)S(1)}, u32[]{:S(2)}) copy-start(bf16[128,16,1152]{2,1,0:T(8,128)(2,1)S(1)} %all_to_all.10) | copy-start | bytes 14155780
  130.6 55.4 %copy-start.10 = (bf16[1024,512]{1,0:T(8,128)(2,1)S(1)}, bf16[1024,512]{1,0:T(8,128)(2,1)}, u32[]{:S(2)}) copy-start(bf16[1024,512]{1,0:T(8,128)(2,1)} %constant.43) | copy-start | bytes 3145732
  186.1 2.5 %copy-start.9 = (bf16[1024,512]{1,0:T(8,128)(2,1)S(1)}, bf16[1024,512]{1,0:T(8,128)(2,1)}, u32[]{:S(2)}) copy-start(bf16[1024,512]{1,0:T(8,128)(2,1)} %constant.41) | copy-start | bytes 3145732
  188.5 2.5 %copy-start.8 = (bf16[1024,512]{1,0:T(8,128)(2,1)S(1)}, bf16[1024,512]{1,0:T(8,128)(2,1)}, u32[]{:S(2)}) copy-start(bf16[1024,512]{1,0:T(8,128)(2,1)} %constant.42) | copy-start | bytes 3145732
  191.0 2.9 %copy-start.7 = (bf16[1024,512]{1,0:T(8,128)(2,1)S(1)}, bf16[1024,512]{1,0:T(8,128)(2,1)}, u32[]{:S(2)}) copy-start(bf16[1024,512]{1,0:T(8,128)(2,1)} %constant.40) | copy-start | bytes 3145732
  196.8 4.4 %copy-start.1 = (f32[1,512,512]{2,1,0:T(8,128)S(1)}, f32[1,512,512]{2,1,0:T(8,128)}, u32[]{:S(2)}) copy-start(f32[1,512,512]{2,1,0:T(8,128)} %param.13) | copy-start | bytes 3145732

commit v9 on v7

--- a/solution.py
+++ b/solution.py
@@ -27,7 +27,8 @@
     lines = out_ref.shape[-1]
     hit = line_ref[...] == lax.broadcasted_iota(jnp.int32, (lines, weights.shape[1]), 0)
     spread = jnp.concatenate(
-        [jnp.where(hit, weights[plane : plane + 1, :], 0.0) for plane in range(weights.shape[0])], axis=0
+        [jnp.where(hit, weights[plane : plane + 1, :], jnp.zeros((), weights.dtype)) for plane in range(weights.shape[0])],
+        axis=0,
     )
     volume = jnp.dot(spread.astype(jnp.bfloat16), rows_ref[...], preferred_element_type=jnp.float32)
     volume_high = volume.astype(jnp.bfloat16)
@@ -90,7 +91,7 @@
 
     step_planes = 8
     weight_in = (
-        got[:, 2 * length : 2 * length + planes].T.astype(jnp.float32).reshape(planes // step_planes, step_planes, slot_count)
+        got[:, 2 * length : 2 * length + planes].T.reshape(planes // step_planes, step_planes, slot_count)
     )
     line_in = got[:, 2 * length + planes].astype(jnp.int32).reshape(1, slot_count)
 

time: 190 us -> 190 us (level)
  no operation moved by 1% of the time
where the time goes in v9:
time: 190 us; the launch traced here: 189 us
  blocking collectives  124 us (65%)
  Pallas kernels  26.9 us (14%)
  matrix products  26 us (14%)
  other arithmetic  8.8 us (5%)
  local copies, waits for them, and re-layouts  2.54 us (1%)
    all_to_all x1, blocking collectives, local(): lax.all_to_all(send.reshape(devices_all, capacity, width), ('slab', 'grp'...  69.1 us
    all_to_all x1, blocking collectives, local(): lax.all_to_all(along_x, 'slab', split_axis=0, concat_axis=0, tiled=True)  55.2 us
    pallas_call x1, Pallas kernels, local(): pl.pallas_call(accumulate_and_transform, out_shape=jax.ShapeDtypeStruct((...  26.9 us
    dot_general x1, matrix products, local(): jnp.dot(placing, payload, preferred_element_type=jnp.float32)  6.19 us
    dot_general x2, matrix products, local(): flat = jnp.dot(lhs, z_high[:, columns], preferred_element_type=jnp.float32)  5.79 us
    dot_general x2, matrix products, local(): jnp.dot(lhs, z_low[:, columns], preferred_element_type=jnp.float32)  4.92 us
    another operation x1, other arithmetic, local(): result = jnp.stack(parts)  4.43 us

profile of v9, /device:TPU:0, one launch (start us, length us, event | category | flops | bytes accessed | tf_op | source)
XLA Modules:
  0.0 188.9 jit_solution(11416980275183304145)
XLA Ops:
  0.0 0.8 convert_element_type.49
  0.8 0.8 copy.16
  1.6 0.2 fusion.36
  1.9 0.1 copy.17
  2.0 1.2 fusion.35
  3.2 0.7 multiply_add_fusion
  3.9 3.6 %fusion.31 = f32[1024,512]{1,0:T(8,128)S(1)} fusion(f32[1024,512]{1,0:T(8,128)} %constant.27.clone, f32[1,512,512]{2,1,0:T(8,128)S(1)} %copy-done), kind=kOutput, calls=%fused_computation.32 | convolution fusion | flops 1610612736 | bytes 5242880 | tf_op jit(solution)/shard_map/dot_general | solution.py:62
  7.4 1.9 %fusion.29 = f32[512,1024]{1,0:T(8,128)S(1)} fusion(f32[512,1024]{1,0:T(8,128)S(1)} %copy-done.4, f32[1024,512]{1,0:T(8,128)S(1)} %fusion.31), kind=kOutput, calls=%fused_computation.30 | convolution fusion | flops 1610612736 | bytes 5242880 | tf_op jit(solution)/shard_map/dot_general | solution.py:65
  9.4 2.0 %add_convert_fusion = bf16[512,1024]{1,0:T(8,128)(2,1)S(1)} fusion(f32[512,1024]{1,0:T(8,128)S(1)} %fusion.29, f32[512,1024]{1,0:T(8,128)S(1)} %copy-done.3, f32[1024,512]{1,0:T(8,128)S(1)} %fusion.31), kind=kOutput, calls=%fused_computation.22 | convolution fusion | flops 1611661312 | bytes 6291456 | tf_op jit(solution)/shard_map/dot_general | solution.py:66
  11.5 0.0 copy-start.11
  11.5 1.3 fusion.25
  12.8 0.3 fusion.27
  13.1 6.2 %fusion.1 = bf16[2048,1152]{1,0:T(8,128)(2,1)S(1)} fusion(s32[1024]{0:T(1024)S(1)} %multiply_add_fusion, bf16[1024,128]{1,0:T(8,128)(2,1)S(1)} %fusion.27, bf16[1024,1024]{1,0:T(8,128)(2,1)S(1)} %fusion.25), kind=kOutput, calls=%fused_computation.3 | convolution fusion | flops 4841013248 | bytes 7081984 | tf_op jit(solution)/shard_map/dot_general | solution.py:86
  19.3 69.1 %all_to_all.10 = bf16[128,16,1152]{2,1,0:T(8,128)(2,1)S(1)} all-to-all(bf16[128,16,1152]{2,1,0:T(8,128)(2,1)S(1)} %bitcast.64), channel_id=1, replica_groups=mesh['slab'=32,'grp'=4] {'slab','grp'}, dimensions={0} | all-to-all | bytes 9437184 | tf_op jit(solution)/shard_map/all_to_all | solution.py:88
  88.5 1.5 convert_reduce_fusion
  89.9 0.7 copy-done.2
  90.7 0.8 copy.18
  91.5 26.9 %shard_map.127 = bf16[32,2,16,16,128]{4,3,2,1,0:T(8,128)(2,1)} custom-call(bf16[2,8,2048]{2,1,0:T(8,128)(2,1)} %bitcast.71, s32[1,2048]{1,0:T(1,128)} %bitcast.75, bf16[2048,1152]{1,0:T(8,128)(2,1)} %bitcast.63, bf16[1024,1024]{1,0:T(8,128)(2,1)} %constant.31.clone.inverse_high_ref, bf16[1024,1024]{1,0:T(8,128)(2,1)} %constant.32.clone.inverse_low_ref), custom_call_target="tpu_custom_call" | custom-call | tf_op jit(solution)/shard_map/pallas_call | solution.py:108
  118.4 55.2 %all_to_all.11 = bf16[32,2,16,16,128]{4,3,2,1,0:T(8,128)(2,1)S(1)} all-to-all(bf16[32,2,16,16,128]{4,3,2,1,0:T(8,128)(2,1)} %shard_map.127), channel_id=1, replica_groups=mesh['slab'=32,'grp'=4] {'slab'}, dimensions={0} | all-to-all | bytes 8388608 | tf_op jit(solution)/shard_map/all_to_all | solution.py:121
  173.7 2.5 %fusion.2 = f32[2048,512]{1,0:T(8,128)S(1)} fusion(bf16[1024,512]{1,0:T(8,128)(2,1)S(1)} %copy-done.10, bf16[128,8,16,128]{3,2,1,0:T(8,128)(2,1)S(1)} %bitcast.65), kind=kOutput, calls=%fused_computation.4 | convolution fusion | flops 2147483648 | bytes 9437184 | tf_op jit(solution)/shard_map/dot_general | solution.py:130
  176.2 2.5 %fusion.6 = f32[2048,512]{1,0:T(8,128)S(1)} fusion(bf16[1024,512]{1,0:T(8,128)(2,1)S(1)} %copy-done.9, bf16[128,8,16,128]{3,2,1,0:T(8,128)(2,1)S(1)} %bitcast.66), kind=kOutput, calls=%fused_computation.8 | convolution fusion | flops 2147483648 | bytes 9437184 | tf_op jit(solution)/shard_map/dot_general | solution.py:130
  178.7 2.9 %fusion.14 = f32[2048,512]{1,0:T(8,128)S(1)} fusion(f32[2048,512]{1,0:T(8,128)S(1)} %fusion.2, bf16[1024,512]{1,0:T(8,128)(2,1)S(1)} %copy-done.8, bf16[128,8,16,128]{3,2,1,0:T(8,128)(2,1)S(1)} %bitcast.67), kind=kOutput, calls=%fused_computation.14 | convolution fusion | flops 2148532224 | bytes 13631488 | tf_op jit(solution)/shard_map/dot_general | solution.py:129
  181.6 2.9 %fusion.11 = f32[2048,512]{1,0:T(8,128)S(1)} fusion(f32[2048,512]{1,0:T(8,128)S(1)} %fusion.6, bf16[1024,512]{1,0:T(8,128)(2,1)S(1)} %copy-done.7, bf16[128,8,16,128]{3,2,1,0:T(8,128)(2,1)S(1)} %bitcast.68), kind=kOutput, calls=%fused_computation.13 | convolution fusion | flops 2148532224 | bytes 13631488 | tf_op jit(solution)/shard_map/dot_general | solution.py:129
  184.5 4.4 %pad_maximum_fusion = f32[2,16,128,512]{3,2,1,0:T(8,128)} fusion(f32[1,16,128,512]{3,2,1,0:T(8,128)S(1)} %bitcast.69, f32[1,16,128,512]{3,2,1,0:T(8,128)S(1)} %bitcast.70), kind=kLoop, calls=%fused_computation | loop fusion | flops 2097152 | bytes 16777216 | tf_op jit(solution)/shard_map/stack | solution.py:132
  (28 shorter events, 0.2 us)
Async XLA Ops:
  0.0 3.9 %copy-start = (f32[1,512,512]{2,1,0:T(8,128)S(1)}, f32[1,512,512]{2,1,0:T(8,128)}, u32[]{:S(2)}) copy-start(f32[1,512,512]{2,1,0:T(8,128)} %param.13) | copy-start | bytes 3145732
  1.8 5.6 %copy-start.4 = (f32[512,1024]{1,0:T(8,128)S(1)}, f32[512,1024]{1,0:T(8,128)}, u32[]{:S(2)}) copy-start(f32[512,1024]{1,0:T(8,128)} %constant.28.clone) | copy-start | bytes 6291460
  3.9 5.5 %copy-start.3 = (f32[512,1024]{1,0:T(8,128)S(1)}, f32[512,1024]{1,0:T(8,128)}, u32[]{:S(2)}) copy-start(f32[512,1024]{1,0:T(8,128)} %constant.29.clone) | copy-start | bytes 6291460
  9.4 2.0 %copy-start.6 = (s32[1,1024]{1,0:T(1,128)S(1)}, s32[1,1024]{1,0:T(1,128)}, u32[]{:S(2)}) copy-start(s32[1,1024]{1,0:T(1,128)} %param.14) | copy-start | bytes 12292
  11.5 1.3 copy-start.5
  11.5 1.3 copy-start.11
  88.5 2.2 %copy-start.2 = (bf16[128,16,1152]{2,1,0:T(8,128)(2,1)}, bf16[128,16,1152]{2,1,0:T(8,128)(2,1)S(1)}, u32[]{:S(2)}) copy-start(bf16[128,16,1152]{2,1,0:T(8,128)(2,1)S(1)} %all_to_all.10) | copy-start | bytes 14155780
  118.4 55.2 %copy-start.10 = (bf16[1024,512]{1,0:T(8,128)(2,1)S(1)}, bf16[1024,512]{1,0:T(8,128)(2,1)}, u32[]{:S(2)}) copy-start(bf16[1024,512]{1,0:T(8,128)(2,1)} %constant.43) | copy-start | bytes 3145732
  173.7 2.5 %copy-start.9 = (bf16[1024,512]{1,0:T(8,128)(2,1)S(1)}, bf16[1024,512]{1,0:T(8,128)(2,1)}, u32[]{:S(2)}) copy-start(bf16[1024,512]{1,0:T(8,128)(2,1)} %constant.41) | copy-start | bytes 3145732
  176.2 2.5 %copy-start.8 = (bf16[1024,512]{1,0:T(8,128)(2,1)S(1)}, bf16[1024,512]{1,0:T(8,128)(2,1)}, u32[]{:S(2)}) copy-start(bf16[1024,512]{1,0:T(8,128)(2,1)} %constant.42) | copy-start | bytes 3145732
  178.7 2.9 %copy-start.7 = (bf16[1024,512]{1,0:T(8,128)(2,1)S(1)}, bf16[1024,512]{1,0:T(8,128)(2,1)}, u32[]{:S(2)}) copy-start(bf16[1024,512]{1,0:T(8,128)(2,1)} %constant.40) | copy-start | bytes 3145732
  184.5 4.4 %copy-start.1 = (f32[1,512,512]{2,1,0:T(8,128)S(1)}, f32[1,512,512]{2,1,0:T(8,128)}, u32[]{:S(2)}) copy-start(f32[1,512,512]{2,1,0:T(8,128)} %param.13) | copy-start | bytes 3145732

commit v10 on v9

--- a/solution.py
+++ b/solution.py
@@ -123,12 +123,9 @@
     lhs = pencil.transpose(3, 4, 0, 1, 2).reshape(x_block * lines_per, 2 * length)
     z_table = inverse.reshape(2, slab_count, planes, 2 * length).transpose(1, 0, 2, 3).reshape(2 * length, 2 * length)
     z_high, z_low = halves(z_table)
-    parts = []
-    for part in range(2):
-        columns = slice(part * length, (part + 1) * length)
-        flat = jnp.dot(lhs, z_high[:, columns], preferred_element_type=jnp.float32)
-        flat = flat + jnp.dot(lhs, z_low[:, columns], preferred_element_type=jnp.float32)
-        parts.append(flat.reshape(x_block, lines_per, length))
+    flat = jnp.dot(lhs, z_high, preferred_element_type=jnp.float32)
+    flat = flat + jnp.dot(lhs, z_low, preferred_element_type=jnp.float32)
+    parts = [flat[:, part * length : (part + 1) * length].reshape(x_block, lines_per, length) for part in range(2)]
     result = jnp.stack(parts)
     return result
 

time: 190 us -> 189 us (level)
  matrix products: 26 us -> 23.8 us
  local copies, waits for them, and re-layouts: 2.54 us -> 4.71 us
    dot_general x4 -> x2, matrix products: 10.7 us -> 10.2 us  [the longest x1 5.32 us: local(): flat = jnp.dot(lhs, z_high, preferred_element_type=jnp.float32)]
where the time goes in v10:
time: 189 us; the launch traced here: 187 us
  blocking collectives  124 us (66%)
  Pallas kernels  26.8 us (14%)
  matrix products  23.8 us (13%)
  other arithmetic  7.36 us (4%)
  local copies, waits for them, and re-layouts  4.71 us (2%)
    all_to_all x1, blocking collectives, local(): lax.all_to_all(send.reshape(devices_all, capacity, width), ('slab', 'grp'...  69.1 us
    all_to_all x1, blocking collectives, local(): lax.all_to_all(along_x, 'slab', split_axis=0, concat_axis=0, tiled=True)  55.2 us
    pallas_call x1, Pallas kernels, local(): pl.pallas_call(accumulate_and_transform, out_shape=jax.ShapeDtypeStruct((...  26.8 us
    dot_general x1, matrix products, local(): jnp.dot(placing, payload, preferred_element_type=jnp.float32)  6.18 us
    dot_general x1, matrix products, local(): flat = jnp.dot(lhs, z_high, preferred_element_type=jnp.float32)  5.32 us
    dot_general x1, matrix products, local(): flat = flat + jnp.dot(lhs, z_low, preferred_element_type=jnp.float32)  4.91 us
    another operation x1, other arithmetic, local(): result = jnp.stack(parts)  4.43 us

profile of v10, /device:TPU:0, one launch (start us, length us, event | category | flops | bytes accessed | tf_op | source)
XLA Modules:
  0.0 187.4 jit_solution(8219223187673267431)
XLA Ops:
  0.0 0.8 convert_element_type.49
  0.8 0.8 copy.16
  1.6 0.2 fusion.27
  1.9 0.1 copy.17
  2.0 0.4 fusion.26
  2.4 1.0 copy-done.5
  3.4 1.8 fusion.22
  5.3 0.0 copy-start.3
  5.3 1.9 %fusion.20 = f32[512,1024]{1,0:T(8,128)S(1)} fusion(f32[512,1024]{1,0:T(8,128)S(1)} %copy-done.4, f32[1024,512]{1,0:T(8,128)S(1)} %fusion.22), kind=kOutput, calls=%fused_computation.23 | convolution fusion | flops 1610612736 | bytes 5242880 | tf_op jit(solution)/shard_map/dot_general | solution.py:65
  7.3 2.0 %add_convert_fusion = bf16[512,1024]{1,0:T(8,128)(2,1)S(1)} fusion(f32[512,1024]{1,0:T(8,128)S(1)} %fusion.20, f32[512,1024]{1,0:T(8,128)S(1)} %copy-done.3, f32[1024,512]{1,0:T(8,128)S(1)} %fusion.22), kind=kOutput, calls=%fused_computation.15 | convolution fusion | flops 1611661312 | bytes 6291456 | tf_op jit(solution)/shard_map/dot_general | solution.py:66
  9.3 0.0 copy-start.11
  9.3 1.3 fusion.16
  10.7 0.3 fusion.18
  11.0 6.2 %fusion.1 = bf16[2048,1152]{1,0:T(8,128)(2,1)S(1)} fusion(s32[1024]{0:T(1024)S(1)} %multiply_add_fusion, bf16[1024,128]{1,0:T(8,128)(2,1)S(1)} %fusion.18, bf16[1024,1024]{1,0:T(8,128)(2,1)S(1)} %fusion.16), kind=kOutput, calls=%fused_computation.3 | convolution fusion | flops 4841013248 | bytes 7081984 | tf_op jit(solution)/shard_map/dot_general | solution.py:86
  17.2 69.1 %all_to_all.10 = bf16[128,16,1152]{2,1,0:T(8,128)(2,1)S(1)} all-to-all(bf16[128,16,1152]{2,1,0:T(8,128)(2,1)S(1)} %bitcast.58), channel_id=1, replica_groups=mesh['slab'=32,'grp'=4] {'slab','grp'}, dimensions={0} | all-to-all | bytes 9437184 | tf_op jit(solution)/shard_map/all_to_all | solution.py:88
  86.3 1.5 convert_reduce_fusion
  87.8 0.7 copy-done.2
  88.5 0.8 copy.18
  89.3 26.8 %shard_map.127 = bf16[32,2,16,16,128]{4,3,2,1,0:T(8,128)(2,1)} custom-call(bf16[2,8,2048]{2,1,0:T(8,128)(2,1)} %bitcast.61, s32[1,2048]{1,0:T(1,128)} %bitcast.65, bf16[2048,1152]{1,0:T(8,128)(2,1)} %bitcast.55, bf16[1024,1024]{1,0:T(8,128)(2,1)} %constant.31.clone.inverse_high_ref, bf16[1024,1024]{1,0:T(8,128)(2,1)} %constant.32.clone.inverse_low_ref), custom_call_target="tpu_custom_call" | custom-call | tf_op jit(solution)/shard_map/pallas_call | solution.py:108
  116.2 55.2 %all_to_all.11 = bf16[32,2,16,16,128]{4,3,2,1,0:T(8,128)(2,1)S(1)} all-to-all(bf16[32,2,16,16,128]{4,3,2,1,0:T(8,128)(2,1)} %shard_map.127), channel_id=1, replica_groups=mesh['slab'=32,'grp'=4] {'slab'}, dimensions={0} | all-to-all | bytes 8388608 | tf_op jit(solution)/shard_map/all_to_all | solution.py:121
  171.4 4.9 %fusion.2 = f32[2048,1024]{1,0:T(8,128)S(1)} fusion(bf16[1024,1024]{1,0:T(8,128)(2,1)S(1)} %copy-done.10, bf16[128,8,16,128]{3,2,1,0:T(8,128)(2,1)S(1)} %bitcast.59), kind=kOutput, calls=%fused_computation.4 | convolution fusion | flops 4294967296 | bytes 14680064 | tf_op jit(solution)/shard_map/dot_general | solution.py:127
  176.4 5.3 %fusion.7 = f32[2048,1024]{1,0:T(8,128)S(1)} fusion(f32[2048,1024]{1,0:T(8,128)S(1)} %fusion.2, bf16[1024,1024]{1,0:T(8,128)(2,1)S(1)} %copy-done.9, bf16[128,8,16,128]{3,2,1,0:T(8,128)(2,1)S(1)} %bitcast.60), kind=kOutput, calls=%fused_computation.9 | convolution fusion | flops 4297064448 | bytes 23068672 | tf_op jit(solution)/shard_map/dot_general | solution.py:126
  181.7 1.2 fusion.32
  182.9 4.4 %pad_maximum_fusion = f32[2,16,128,512]{3,2,1,0:T(8,128)} fusion(f32[1,16,128,512]{3,2,1,0:T(8,128)S(1)} %bitcast.57, f32[1,16,128,512]{3,2,1,0:T(8,128)S(1)} %bitcast.56), kind=kLoop, calls=%fused_computation | loop fusion | flops 2097152 | bytes 16777216 | tf_op jit(solution)/shard_map/stack | solution.py:129
  (27 shorter events, 0.2 us)
Async XLA Ops:
  0.0 2.4 %copy-start = (f32[1,512,512]{2,1,0:T(8,128)S(1)}, f32[1,512,512]{2,1,0:T(8,128)}, u32[]{:S(2)}) copy-start(f32[1,512,512]{2,1,0:T(8,128)} %param.13) | copy-start | bytes 3145732
  0.0 2.0 %copy-start.6 = (s32[1,1024,1]{1,2,0:T(1,128)S(1)}, s32[1,1024,1]{1,2,0:T(1,128)}, u32[]{:S(2)}) copy-start(s32[1,1024,1]{1,2,0:T(1,128)} %param.15) | copy-start | bytes 12292
  1.8 1.6 copy-start.5
  3.4 1.9 copy-start.4
  5.3 2.0 %copy-start.3 = (f32[512,1024]{1,0:T(8,128)S(1)}, f32[512,1024]{1,0:T(8,128)}, u32[]{:S(2)}) copy-start(f32[512,1024]{1,0:T(8,128)} %constant.29.clone) | copy-start | bytes 6291460
  7.3 2.0 %copy-start.8 = (s32[1,1024]{1,0:T(1,128)S(1)}, s32[1,1024]{1,0:T(1,128)}, u32[]{:S(2)}) copy-start(s32[1,1024]{1,0:T(1,128)} %param.14) | copy-start | bytes 12292
  9.3 1.3 copy-start.7
  9.3 1.3 copy-start.11
  86.3 2.2 %copy-start.2 = (bf16[128,16,1152]{2,1,0:T(8,128)(2,1)}, bf16[128,16,1152]{2,1,0:T(8,128)(2,1)S(1)}, u32[]{:S(2)}) copy-start(bf16[128,16,1152]{2,1,0:T(8,128)(2,1)S(1)} %all_to_all.10) | copy-start | bytes 14155780
  116.2 55.2 %copy-start.10 = (bf16[1024,1024]{1,0:T(8,128)(2,1)S(1)}, bf16[1024,1024]{1,0:T(8,128)(2,1)}, u32[]{:S(2)}) copy-start(bf16[1024,1024]{1,0:T(8,128)(2,1)} %constant.34.clone) | copy-start | bytes 6291460
  171.4 4.9 %copy-start.9 = (bf16[1024,1024]{1,0:T(8,128)(2,1)S(1)}, bf16[1024,1024]{1,0:T(8,128)(2,1)}, u32[]{:S(2)}) copy-start(bf16[1024,1024]{1,0:T(8,128)(2,1)} %constant.33.clone) | copy-start | bytes 6291460
  182.9 4.4 %copy-start.1 = (f32[1,512,512]{2,1,0:T(8,128)S(1)}, f32[1,512,512]{2,1,0:T(8,128)}, u32[]{:S(2)}) copy-start(f32[1,512,512]{2,1,0:T(8,128)} %param.13) | copy-start | bytes 3145732

commit v11 on v10

--- a/solution.py
+++ b/solution.py
@@ -22,7 +22,7 @@
     return jnp.asarray(high), jnp.asarray(low)
 
 
-def accumulate_and_transform(weight_ref, line_ref, rows_ref, inverse_high_ref, inverse_low_ref, out_ref):
+def accumulate_and_transform(weight_ref, line_ref, rows_ref, inverse_ref, out_ref):
     weights = weight_ref[0]
     lines = out_ref.shape[-1]
     hit = line_ref[...] == lax.broadcasted_iota(jnp.int32, (lines, weights.shape[1]), 0)
@@ -33,10 +33,8 @@
     volume = jnp.dot(spread.astype(jnp.bfloat16), rows_ref[...], preferred_element_type=jnp.float32)
     volume_high = volume.astype(jnp.bfloat16)
     volume_low = (volume - volume_high.astype(jnp.float32)).astype(jnp.bfloat16)
-    contract = (((1,), (1,)), ((), ()))
-    along = lax.dot_general(inverse_high_ref[...], volume_high, contract, preferred_element_type=jnp.float32)
-    along = along + lax.dot_general(inverse_high_ref[...], volume_low, contract, preferred_element_type=jnp.float32)
-    along = along + lax.dot_general(inverse_low_ref[...], volume_high, contract, preferred_element_type=jnp.float32)
+    stacked = jnp.concatenate([volume_high, volume_low, volume_high], axis=1)
+    along = lax.dot_general(inverse_ref[...], stacked, (((1,), (1,)), ((), ())), preferred_element_type=jnp.float32)
     blocks, _, parts, x_in, lanes = out_ref.shape
     for part in range(parts):
         piece = along[:, part * lanes : (part + 1) * lanes].reshape(blocks, 2, x_in, lanes)
@@ -113,11 +111,10 @@
             pl.BlockSpec((1, step_planes, slot_count), lambda i: (i, 0, 0)),
             pl.BlockSpec((1, slot_count), lambda i: (0, 0)),
             pl.BlockSpec((slot_count, 2 * length), lambda i: (0, 0)),
-            pl.BlockSpec((2 * length, 2 * length), lambda i: (0, 0)),
-            pl.BlockSpec((2 * length, 2 * length), lambda i: (0, 0)),
+            pl.BlockSpec((2 * length, 6 * length), lambda i: (0, 0)),
         ],
         out_specs=pl.BlockSpec((slab_count, 2, step_planes, x_block, lines_per), lambda i: (0, 0, i, 0, 0)),
-    )(weight_in, line_in, got, inverse_high, inverse_low)
+    )(weight_in, line_in, got, jnp.concatenate([inverse_high, inverse_high, inverse_low], axis=1))
     pencil = lax.all_to_all(along_x, "slab", split_axis=0, concat_axis=0, tiled=True)
 
     lhs = pencil.transpose(3, 4, 0, 1, 2).reshape(x_block * lines_per, 2 * length)

time: 189 us -> 189 us (level)
  no operation moved by 1% of the time
where the time goes in v11:
time: 189 us; the launch traced here: 188 us
  blocking collectives  124 us (66%)
  Pallas kernels  27.4 us (14%)
  matrix products  23.8 us (13%)
  other arithmetic  7.36 us (4%)
  local copies, waits for them, and re-layouts  4.71 us (2%)
    all_to_all x1, blocking collectives, local(): lax.all_to_all(send.reshape(devices_all, capacity, width), ('slab', 'grp'...  69.1 us
    all_to_all x1, blocking collectives, local(): lax.all_to_all(along_x, 'slab', split_axis=0, concat_axis=0, tiled=True)  55.2 us
    pallas_call x1, Pallas kernels, local(): pl.pallas_call(accumulate_and_transform, out_shape=jax.ShapeDtypeStruct((...  27.4 us
    dot_general x1, matrix products, local(): jnp.dot(placing, payload, preferred_element_type=jnp.float32)  6.18 us
    dot_general x1, matrix products, local(): flat = jnp.dot(lhs, z_high, preferred_element_type=jnp.float32)  5.32 us
    dot_general x1, matrix products, local(): flat = flat + jnp.dot(lhs, z_low, preferred_element_type=jnp.float32)  4.9 us
    another operation x1, other arithmetic, local(): result = jnp.stack(parts)  4.43 us

profile of v11, /device:TPU:0, one launch (start us, length us, event | category | flops | bytes accessed | tf_op | source)
XLA Modules:
  0.0 187.9 jit_solution(12586893232839294608)
XLA Ops:
  0.0 0.8 convert_element_type.49
  0.8 0.8 copy.16
  1.6 0.2 fusion.27
  1.9 0.1 copy.17
  2.0 0.4 fusion.26
  2.4 1.0 copy-done.5
  3.4 1.8 fusion.22
  5.3 0.0 copy-start.3
  5.3 1.9 %fusion.20 = f32[512,1024]{1,0:T(8,128)S(1)} fusion(f32[512,1024]{1,0:T(8,128)S(1)} %copy-done.4, f32[1024,512]{1,0:T(8,128)S(1)} %fusion.22), kind=kOutput, calls=%fused_computation.23 | convolution fusion | flops 1610612736 | bytes 5242880 | tf_op jit(solution)/shard_map/dot_general | solution.py:63
  7.3 2.0 %add_convert_fusion = bf16[512,1024]{1,0:T(8,128)(2,1)S(1)} fusion(f32[512,1024]{1,0:T(8,128)S(1)} %fusion.20, f32[512,1024]{1,0:T(8,128)S(1)} %copy-done.3, f32[1024,512]{1,0:T(8,128)S(1)} %fusion.22), kind=kOutput, calls=%fused_computation.15 | convolution fusion | flops 1611661312 | bytes 6291456 | tf_op jit(solution)/shard_map/dot_general | solution.py:64
  9.3 0.0 copy-start.11
  9.3 1.3 fusion.16
  10.7 0.3 fusion.18
  11.0 6.2 %fusion.1 = bf16[2048,1152]{1,0:T(8,128)(2,1)S(1)} fusion(s32[1024]{0:T(1024)S(1)} %multiply_add_fusion, bf16[1024,128]{1,0:T(8,128)(2,1)S(1)} %fusion.18, bf16[1024,1024]{1,0:T(8,128)(2,1)S(1)} %fusion.16), kind=kOutput, calls=%fused_computation.3 | convolution fusion | flops 4841013248 | bytes 7081984 | tf_op jit(solution)/shard_map/dot_general | solution.py:84
  17.2 69.1 %all_to_all.10 = bf16[128,16,1152]{2,1,0:T(8,128)(2,1)S(1)} all-to-all(bf16[128,16,1152]{2,1,0:T(8,128)(2,1)S(1)} %bitcast.58), channel_id=1, replica_groups=mesh['slab'=32,'grp'=4] {'slab','grp'}, dimensions={0} | all-to-all | bytes 9437184 | tf_op jit(solution)/shard_map/all_to_all | solution.py:86
  86.3 1.5 convert_reduce_fusion
  87.8 0.7 copy-done.2
  88.5 0.8 copy.18
  89.3 27.4 %shard_map.127 = bf16[32,2,16,16,128]{4,3,2,1,0:T(8,128)(2,1)} custom-call(bf16[2,8,2048]{2,1,0:T(8,128)(2,1)} %bitcast.61, s32[1,2048]{1,0:T(1,128)} %bitcast.65, bf16[2048,1152]{1,0:T(8,128)(2,1)} %bitcast.55, bf16[1024,3072]{1,0:T(8,128)(2,1)} %constant.40.inverse_ref), custom_call_target="tpu_custom_call" | custom-call | tf_op jit(solution)/shard_map/pallas_call | solution.py:106
  116.7 55.2 %all_to_all.11 = bf16[32,2,16,16,128]{4,3,2,1,0:T(8,128)(2,1)S(1)} all-to-all(bf16[32,2,16,16,128]{4,3,2,1,0:T(8,128)(2,1)} %shard_map.127), channel_id=1, replica_groups=mesh['slab'=32,'grp'=4] {'slab'}, dimensions={0} | all-to-all | bytes 8388608 | tf_op jit(solution)/shard_map/all_to_all | solution.py:118
  172.0 4.9 %fusion.2 = f32[2048,1024]{1,0:T(8,128)S(1)} fusion(bf16[1024,1024]{1,0:T(8,128)(2,1)S(1)} %copy-done.10, bf16[128,8,16,128]{3,2,1,0:T(8,128)(2,1)S(1)} %bitcast.59), kind=kOutput, calls=%fused_computation.4 | convolution fusion | flops 4294967296 | bytes 14680064 | tf_op jit(solution)/shard_map/dot_general | solution.py:124
  176.9 5.3 %fusion.7 = f32[2048,1024]{1,0:T(8,128)S(1)} fusion(f32[2048,1024]{1,0:T(8,128)S(1)} %fusion.2, bf16[1024,1024]{1,0:T(8,128)(2,1)S(1)} %copy-done.9, bf16[128,8,16,128]{3,2,1,0:T(8,128)(2,1)S(1)} %bitcast.60), kind=kOutput, calls=%fused_computation.9 | convolution fusion | flops 4297064448 | bytes 23068672 | tf_op jit(solution)/shard_map/dot_general | solution.py:123
  182.2 1.2 fusion.32
  183.4 4.4 %pad_maximum_fusion = f32[2,16,128,512]{3,2,1,0:T(8,128)} fusion(f32[1,16,128,512]{3,2,1,0:T(8,128)S(1)} %bitcast.57, f32[1,16,128,512]{3,2,1,0:T(8,128)S(1)} %bitcast.56), kind=kLoop, calls=%fused_computation | loop fusion | flops 2097152 | bytes 16777216 | tf_op jit(solution)/shard_map/stack | solution.py:126
  (27 shorter events, 0.2 us)
Async XLA Ops:
  0.0 2.4 %copy-start = (f32[1,512,512]{2,1,0:T(8,128)S(1)}, f32[1,512,512]{2,1,0:T(8,128)}, u32[]{:S(2)}) copy-start(f32[1,512,512]{2,1,0:T(8,128)} %param.13) | copy-start | bytes 3145732
  0.0 2.0 %copy-start.6 = (s32[1,1024,1]{1,2,0:T(1,128)S(1)}, s32[1,1024,1]{1,2,0:T(1,128)}, u32[]{:S(2)}) copy-start(s32[1,1024,1]{1,2,0:T(1,128)} %param.15) | copy-start | bytes 12292
  1.8 1.6 copy-start.5
  3.4 1.9 copy-start.4
  5.3 2.0 %copy-start.3 = (f32[512,1024]{1,0:T(8,128)S(1)}, f32[512,1024]{1,0:T(8,128)}, u32[]{:S(2)}) copy-start(f32[512,1024]{1,0:T(8,128)} %constant.29.clone) | copy-start | bytes 6291460
  7.3 2.0 %copy-start.8 = (s32[1,1024]{1,0:T(1,128)S(1)}, s32[1,1024]{1,0:T(1,128)}, u32[]{:S(2)}) copy-start(s32[1,1024]{1,0:T(1,128)} %param.14) | copy-start | bytes 12292
  9.3 1.3 copy-start.7
  9.3 1.3 copy-start.11
  86.3 2.2 %copy-start.2 = (bf16[128,16,1152]{2,1,0:T(8,128)(2,1)}, bf16[128,16,1152]{2,1,0:T(8,128)(2,1)S(1)}, u32[]{:S(2)}) copy-start(bf16[128,16,1152]{2,1,0:T(8,128)(2,1)S(1)} %all_to_all.10) | copy-start | bytes 14155780
  116.7 55.2 %copy-start.10 = (bf16[1024,1024]{1,0:T(8,128)(2,1)S(1)}, bf16[1024,1024]{1,0:T(8,128)(2,1)}, u32[]{:S(2)}) copy-start(bf16[1024,1024]{1,0:T(8,128)(2,1)} %constant.34.clone) | copy-start | bytes 6291460
  172.0 4.9 %copy-start.9 = (bf16[1024,1024]{1,0:T(8,128)(2,1)S(1)}, bf16[1024,1024]{1,0:T(8,128)(2,1)}, u32[]{:S(2)}) copy-start(bf16[1024,1024]{1,0:T(8,128)(2,1)} %constant.33.clone) | copy-start | bytes 6291460
  183.4 4.4 %copy-start.1 = (f32[1,512,512]{2,1,0:T(8,128)S(1)}, f32[1,512,512]{2,1,0:T(8,128)}, u32[]{:S(2)}) copy-start(f32[1,512,512]{2,1,0:T(8,128)} %param.13) | copy-start | bytes 3145732
